TPU v7x, 32 devices: a whole 2x2x4 slice. The times are simulated.
32 devices in a mesh: dp: 8 (over y, x, core), tensor: 4 (over z).
Axes of the slice: x: 2, y: 2, z: 4, core: 2. Of those that a mesh axis runs over, the one named last changes fastest.
Arguments:
- hidden_in: bfloat16 [16, 1024, 2048], P('dp', 'tensor'), may hold values from -6 to 6
- keep_slot: int32 [16], P('dp'), may hold values 0 or 1
- out_grad: bfloat16 [16, 1024, 2048], P('dp', 'tensor'), may hold values from -8 to 8
- ln1_gain: bfloat16 [2048], replicated, may hold values from 0.5 to 1.5
- ln1_bias: bfloat16 [2048], replicated, may hold values from -1.25 to 1.25
- ln2_gain: bfloat16 [2048], replicated, may hold values from 0.5 to 1.5
- ln2_bias: bfloat16 [2048], replicated, may hold values from -1.25 to 1.25
- qkv_weight: bfloat16 [2048, 6144], P(None, 'tensor'), may hold values from -0.125 to 0.125
- qkv_bias: bfloat16 [8, 768], P('tensor'), may hold values from -0.625 to 0.625
- dense_weight: bfloat16 [2048, 2048], P('tensor'), may hold values from -0.75 to 0.75
- dense_bias: bfloat16 [2048], replicated, may hold values from -1.25 to 1.25
- fc1_weight: bfloat16 [2048, 8192], P(None, 'tensor'), may hold values from -0.125 to 0.125
- fc1_bias: bfloat16 [8192], P('tensor'), may hold values from -1.25 to 1.25
- fc2_weight: bfloat16 [8192, 2048], P('tensor'), may hold values from -0.0625 to 0.0625
- fc2_bias: bfloat16 [2048], replicated, may hold values from -1.25 to 1.25
Outputs:
- block_out: bfloat16 [16, 1024, 2048], P('dp', 'tensor')
- hidden_grad: float32 [16, 1024, 2048], P('dp', 'tensor')
- ln1_gain_grad: float32 [2048], P(('dp', 'tensor'))
- ln1_bias_grad: float32 [2048], P(('dp', 'tensor'))
- ln2_gain_grad: float32 [2048], P(('dp', 'tensor'))
- ln2_bias_grad: float32 [2048], P(('dp', 'tensor'))
- qkv_weight_grad: float32 [2048, 6144], P('dp', 'tensor')
- qkv_bias_grad: float32 [8, 768], P('tensor', 'dp')
- dense_weight_grad: float32 [2048, 2048], P('tensor', 'dp')
- dense_bias_grad: float32 [2048], P(('dp', 'tensor'))
- fc1_weight_grad: float32 [2048, 8192], P('dp', 'tensor')
- fc1_bias_grad: float32 [4, 2048], P('tensor', 'dp')
- fc2_weight_grad: float32 [8192, 2048], P('tensor', 'dp')
- fc2_bias_grad: float32 [2048], P(('dp', 'tensor'))
All inputs are finite; a program needn't handle non-finite values. No bound on the sum of `keep_slot` on one device may be relied on, other than what follows from the above.
Results may differ from a plain program's by a relative error of at most 0.0092.
Values may be sent and summed in bfloat16 or wider, within the bound.
No kernel may reach another device: no remote copies, remote signals or barrier semaphores. Data moves between devices by JAX's collectives and lax.ppermute only.
A program may use at most 320 MiB of HBM per device.

v0:
```python
import math

import jax
import jax.numpy as jnp
from jax import lax
from jax.sharding import PartitionSpec as P

ROT = 64


layer_eps = 1e-05
rope_base = 10000.0
mask_fill = -1e30
block_rows = 512


def rope_tables(length, rot_dims):
    half = rot_dims // 2
    freqs = jnp.exp(-jnp.log(rope_base) * (2.0 * jnp.arange(half, dtype=jnp.float32) / rot_dims))
    angles = jnp.arange(length, dtype=jnp.float32)[:, None] * freqs[None, :]
    return (jnp.cos(angles), jnp.sin(angles))


def rotate(field, cosine, sine, rot_dims, sign):
    half = rot_dims // 2
    first = field[..., :half]
    second = field[..., half:rot_dims]
    rest = field[..., rot_dims:]
    cos_b = cosine[:, None, :]
    sin_b = sign * sine[:, None, :]
    return jnp.concatenate(
        [first * cos_b - second * sin_b, second * cos_b + first * sin_b, rest], axis=-1
    )


def gelu_exact(field):
    return jax.nn.gelu(field, approximate=False)


def contract_rows(left, right):
    return lax.dot_general(
        left, right, (((0,), (0,)), ((), ())), preferred_element_type=jnp.float32
    )


def contract_cols(left, right):
    return lax.dot_general(
        left, right, (((1,), (1,)), ((), ())), preferred_element_type=jnp.float32
    )


def local(
    hidden_in,
    keep_slot,
    out_grad,
    ln1_gain,
    ln1_bias,
    ln2_gain,
    ln2_bias,
    qkv_weight,
    qkv_bias,
    dense_weight,
    dense_bias,
    fc1_weight,
    fc1_bias,
    fc2_weight,
    fc2_bias,
):
    slot_count, own_len, width = hidden_in.shape
    seq_len = own_len * lax.axis_size("tensor")
    head_local, three_hd = qkv_bias.shape
    head_dim = three_hd // 3
    scale = 1.0 / math.sqrt(head_dim)
    start_row = lax.axis_index("tensor") * own_len
    inputs_all, grads_all = (
        lax.all_gather(hidden_in, "tensor", axis=1, tiled=True),
        lax.all_gather(out_grad, "tensor", axis=1, tiled=True),
    )
    cosine, sine = rope_tables(seq_len, ROT)
    blk = min(block_rows, seq_len)
    n_blocks = seq_len // blk
    key_pos = jnp.arange(seq_len)
    starts = jnp.arange(n_blocks) * blk
    qkv_acc = jnp.zeros(qkv_weight.shape, jnp.float32)
    dense_acc = jnp.zeros(dense_weight.shape, jnp.float32)
    up_acc = jnp.zeros(fc1_weight.shape, jnp.float32)
    down_acc = jnp.zeros(fc2_weight.shape, jnp.float32)
    qkv_bias_acc = jnp.zeros((head_local * three_hd,), jnp.float32)
    up_bias_acc = jnp.zeros(fc1_bias.shape, jnp.float32)
    gain_one_acc = jnp.zeros((width,), jnp.float32)
    shift_one_acc = jnp.zeros((width,), jnp.float32)
    gain_two_acc = jnp.zeros((width,), jnp.float32)
    shift_two_acc = jnp.zeros((width,), jnp.float32)
    out_bias_acc = jnp.zeros((width,), jnp.float32)
    out_rows = []
    grad_rows_out = []
    for slot_idx in range(slot_count):
        keep = keep_slot[slot_idx].astype(jnp.float32)
        rows_full = inputs_all[slot_idx].astype(jnp.float32)
        centred = rows_full - jnp.mean(rows_full, axis=-1, keepdims=True)
        inv_std = lax.rsqrt(jnp.mean(centred * centred, axis=-1, keepdims=True) + layer_eps)
        normed = centred * inv_std
        normed_one = (normed * ln1_gain + ln1_bias).astype(jnp.bfloat16)
        normed_two = (normed * ln2_gain + ln2_bias).astype(jnp.bfloat16)
        joined = jnp.dot(
            normed_one, qkv_weight, preferred_element_type=jnp.float32
        ) + qkv_bias.reshape(-1)
        joined = joined.reshape(seq_len, head_local, 3, head_dim)
        query_rot = rotate(joined[:, :, 0], cosine, sine, ROT, 1.0).astype(jnp.bfloat16)
        key_rot = rotate(joined[:, :, 1], cosine, sine, ROT, 1.0).astype(jnp.bfloat16)
        value_rows = joined[:, :, 2].astype(jnp.bfloat16)
        query_blocks = query_rot.reshape(n_blocks, blk, head_local, head_dim)

        def block_scores(query_blk, blk_start):
            scores = (
                jnp.einsum("bhd,khd->hbk", query_blk, key_rot, preferred_element_type=jnp.float32)
                * scale
            )
            allowed = key_pos[None, :] <= (blk_start + jnp.arange(blk))[:, None]
            return jnp.where(allowed[None], scores, mask_fill)

        def attend(items):
            query_blk, blk_start = items
            scores = block_scores(query_blk, blk_start)
            top = jnp.max(scores, axis=-1, keepdims=True)
            weights = jnp.exp(scores - top)
            total = jnp.sum(weights, axis=-1, keepdims=True)
            probs = weights / total
            mixed = jnp.einsum(
                "hbk,khd->bhd",
                probs.astype(jnp.bfloat16),
                value_rows,
                preferred_element_type=jnp.float32,
            )
            return (mixed.astype(jnp.bfloat16), (top + jnp.log(total))[..., 0])

        attn_blocks, log_total = lax.map(attend, (query_blocks, starts))
        attn_flat = attn_blocks.reshape(seq_len, head_local * head_dim)
        pre_act = jnp.dot(normed_two, fc1_weight, preferred_element_type=jnp.float32) + fc1_bias
        act_val, act_back = jax.vjp(gelu_exact, pre_act)
        act_low = act_val.astype(jnp.bfloat16)
        partial_out = jnp.dot(
            attn_flat, dense_weight, preferred_element_type=jnp.float32
        ) + jnp.dot(act_low, fc2_weight, preferred_element_type=jnp.float32)
        summed = lax.psum(partial_out, "tensor")
        branch_own = lax.dynamic_slice_in_dim(summed, start_row, own_len, 0)
        branch_own = branch_own + dense_bias + fc2_bias
        own_in = hidden_in[slot_idx].astype(jnp.float32)
        out_rows.append((own_in + keep * branch_own).astype(jnp.bfloat16))
        branch_grad = grads_all[slot_idx] * keep_slot[slot_idx].astype(jnp.bfloat16)
        own_cot = out_grad[slot_idx].astype(jnp.float32)
        out_bias_acc = out_bias_acc + jnp.sum(own_cot * keep, axis=0)
        down_acc = down_acc + contract_rows(act_low, branch_grad)
        dense_acc = dense_acc + contract_rows(attn_flat, branch_grad)
        act_grad = contract_cols(branch_grad, fc2_weight)
        pre_grad = act_back(act_grad)[0].astype(jnp.bfloat16)
        up_bias_acc = up_bias_acc + jnp.sum(pre_grad.astype(jnp.float32), axis=0)
        up_acc = up_acc + contract_rows(normed_two, pre_grad)
        normed_two_grad = contract_cols(pre_grad, fc1_weight)
        mixed_grad = contract_cols(branch_grad, dense_weight).astype(jnp.bfloat16)
        grad_blocks = mixed_grad.reshape(n_blocks, blk, head_local, head_dim)

        def attend_back(carry, items):
            key_acc, value_acc = carry
            query_blk, grad_blk, lse_blk, blk_start = items
            scores = block_scores(query_blk, blk_start)
            probs = jnp.exp(scores - lse_blk[..., None])
            probs_low = probs.astype(jnp.bfloat16)
            prob_grad = jnp.einsum(
                "bhd,khd->hbk", grad_blk, value_rows, preferred_element_type=jnp.float32
            )
            inner = jnp.sum(probs * prob_grad, axis=-1, keepdims=True)
            score_grad = (probs * (prob_grad - inner)).astype(jnp.bfloat16)
            query_grad = (
                jnp.einsum("hbk,khd->bhd", score_grad, key_rot, preferred_element_type=jnp.float32)
                * scale
            )
            key_acc = (
                key_acc
                + jnp.einsum(
                    "hbk,bhd->khd", score_grad, query_blk, preferred_element_type=jnp.float32
                )
                * scale
            )
            value_acc = value_acc + jnp.einsum(
                "hbk,bhd->khd", probs_low, grad_blk, preferred_element_type=jnp.float32
            )
            return ((key_acc, value_acc), query_grad)

        empty = jnp.zeros((seq_len, head_local, head_dim), jnp.float32)
        (key_grad, value_grad), query_grad = lax.scan(
            attend_back, (empty, empty), (query_blocks, grad_blocks, log_total, starts)
        )
        query_grad = rotate(
            query_grad.reshape(seq_len, head_local, head_dim), cosine, sine, ROT, -1.0
        )
        key_grad = rotate(key_grad, cosine, sine, ROT, -1.0)
        joined_grad = (
            jnp.stack([query_grad, key_grad, value_grad], axis=2)
            .reshape(seq_len, head_local * three_hd)
            .astype(jnp.bfloat16)
        )
        qkv_bias_acc = qkv_bias_acc + jnp.sum(joined_grad.astype(jnp.float32), axis=0)
        qkv_acc = qkv_acc + contract_rows(normed_one, joined_grad)
        normed_one_grad = contract_cols(joined_grad, qkv_weight)
        gain_one_acc = gain_one_acc + jnp.sum(normed_one_grad * normed, axis=0)
        shift_one_acc = shift_one_acc + jnp.sum(normed_one_grad, axis=0)
        gain_two_acc = gain_two_acc + jnp.sum(normed_two_grad * normed, axis=0)
        shift_two_acc = shift_two_acc + jnp.sum(normed_two_grad, axis=0)
        normed_grad = normed_one_grad * ln1_gain + normed_two_grad * ln2_gain
        grad_summed = lax.psum(normed_grad.astype(jnp.bfloat16), "tensor").astype(jnp.float32)
        own_grad = lax.dynamic_slice_in_dim(grad_summed, start_row, own_len, 0)
        own_normed = lax.dynamic_slice_in_dim(normed, start_row, own_len, 0)
        own_inv = lax.dynamic_slice_in_dim(inv_std, start_row, own_len, 0)
        back_rows = own_inv * (
            own_grad
            - jnp.mean(own_grad, axis=-1, keepdims=True)
            - own_normed * jnp.mean(own_grad * own_normed, axis=-1, keepdims=True)
        )
        grad_rows_out.append(own_cot + back_rows)
    weight_parts = (
        lax.psum_scatter(qkv_acc, "dp", scatter_dimension=0, tiled=True),
        lax.psum_scatter(dense_acc, "dp", scatter_dimension=1, tiled=True),
        lax.psum_scatter(up_acc, "dp", scatter_dimension=0, tiled=True),
        lax.psum_scatter(down_acc, "dp", scatter_dimension=1, tiled=True),
        lax.psum_scatter(
            qkv_bias_acc.reshape(head_local, three_hd), "dp", scatter_dimension=1, tiled=True
        ),
        lax.psum_scatter(up_bias_acc.reshape(1, -1), "dp", scatter_dimension=1, tiled=True),
    )
    small_parts = lax.psum_scatter(
        jnp.stack([gain_one_acc, shift_one_acc, gain_two_acc, shift_two_acc, out_bias_acc]),
        ("dp", "tensor"),
        scatter_dimension=1,
        tiled=True,
    )
    block_out = jnp.stack(out_rows)
    hidden_grad = jnp.stack(grad_rows_out)
    return (
        block_out,
        hidden_grad,
        small_parts[0],
        small_parts[1],
        small_parts[2],
        small_parts[3],
        weight_parts[0],
        weight_parts[4],
        weight_parts[1],
        small_parts[4],
        weight_parts[2],
        weight_parts[5],
        weight_parts[3],
        small_parts[4],
    )


def solution(mesh):
    in_specs = (
        P("dp", "tensor", None),
        P("dp"),
        P("dp", "tensor", None),
        P(),
        P(),
        P(),
        P(),
        P(None, "tensor"),
        P("tensor", None),
        P("tensor", None),
        P(),
        P(None, "tensor"),
        P("tensor"),
        P("tensor", None),
        P(),
    )
    out_specs = (
        P("dp", "tensor", None),
        P("dp", "tensor", None),
        P(("dp", "tensor")),
        P(("dp", "tensor")),
        P(("dp", "tensor")),
        P(("dp", "tensor")),
        P("dp", "tensor"),
        P("tensor", "dp"),
        P("tensor", "dp"),
        P(("dp", "tensor")),
        P("dp", "tensor"),
        P("tensor", "dp"),
        P("tensor", "dp"),
        P(("dp", "tensor")),
    )
    return jax.shard_map(local, mesh=mesh, in_specs=in_specs, out_specs=out_specs, check_vma=False)
```

profile of v0, /device:TPU:0, one launch (start us, length us, event | category | flops | bytes accessed | tf_op | source)
XLA Modules:
  0.0 2166.4 jit_solution(5631583935324290304)
XLA Ops:
  13.9 148.1 %all-gather.3.cloned.1.call-done = bf16[2,1024,2048]{2,1,0:T(8,128)(2,1)} async-done(((bf16[2,256,2048]{2,1,0:T(8,128)(2,1)}), bf16[2,1024,2048]{2,1,0:T(8,128)(2,1)}) %all-gather.3.cloned.1.call-update) | async-done | bytes 8388624 | tf_op jit(solution)/shard_map/all_gather | solution.py:76
  187.7 12.4 convolution_add_fusion.3
  236.9 17.1 while.57
  254.0 57.4 %all-gather.5.cloned.1.call-done = bf16[2,1024,2048]{2,1,0:T(8,128)(2,1)} async-done(((bf16[2,256,2048]{2,1,0:T(8,128)(2,1)}), bf16[2,1024,2048]{2,1,0:T(8,128)(2,1)}) %all-gather.5.cloned.1.call-update) | async-done | bytes 8388624 | tf_op jit(solution)/shard_map/all_gather | solution.py:77
  319.1 41.9 %while.59 = (s32[]{:T(128)}, f32[1024,2,256]{0,2,1:T(8,128)}, f32[1024,2,256]{0,2,1:T(8,128)}, f32[2,512,2,256]{3,1,0,2:T(8,128)}, bf16[2,512,2,256]{3,1,2,0:T(8...) while((s32[]{:T(128)}, f32[1024,2,256]{0,2,1:T(8,128)}, ...), condition=%wide.region_22.23_spmd.clone, body=%wide.region_20.22_spmd.clone.sunk | while | flops 2703490560 | bytes 112231744 | solution.py:191
  385.5 15.8 while.56
  408.9 82.9 %while.58 = (s32[]{:T(128)}, f32[1024,2,256]{0,2,1:T(8,128)}, f32[1024,2,256]{0,2,1:T(8,128)}, f32[2,512,2,256]{1,0,3,2:T(2,128)}, bf16[2,512,2,256]{3,1,2,0:T(8...) while((s32[]{:T(128)}, f32[1024,2,256]{0,2,1:T(8,128)}, ...), condition=%wide.region_16.17_spmd.clone, body=%wide.region_14.16_spmd.clone.sunk | while | flops 2703490560 | bytes 112231848 | solution.py:191
  422.7 19.6 dynamic_update_slice.42
  463.1 19.6 dynamic_update_slice.42
  534.3 11.9 fusion.170
  546.3 10.9 fusion.172
  557.3 11.8 fusion.162
  569.2 50.6 %multiply_convert_fusion.3 = (bf16[1024,2048]{1,0:T(8,128)(2,1)}, f32[1024,2048]{1,0:T(8,128)}, bf16[1024,2048]{1,0:T(8,128)(2,1)}, f32[1024,2048]{1,0:T(8,128)}, f32[1024,2048]{1,0:T(8,128)}) fusion(f32[2048]{0:T(1024)S(1)} %copy-done.52, f32[1024,2048]{1,0:T(8,128)} %fusion.162, bf16[2048,2048]{1,0:T(8,128)(2,1)S(1)} %bitcast.409, ...), kind=kOutput, calls=%fused_computation.149 | convolution fusion | flops 8879341568 | bytes 54558720 | tf_op jit(solution)/shard_map/dot_general | solution.py:139
  619.7 19.0 convert_reduce_fusion.3
  638.7 14.8 fusion.171
  653.5 20.4 convert_reduce_fusion.2
  673.9 29.7 %multiply_reduce_fusion.2 = (f32[2048]{0:T(1024)S(1)}, f32[2048]{0:T(1024)S(1)}, f32[2048]{0:T(1024)S(1)}, f32[2048]{0:T(1024)S(1)}, f32[2048]{0:T(1024)S(1)}, /...) fusion(f32[1024]{0:T(1024)S(1)} %copy-done.55, ...), kind=kOutput, calls=%fused_computation.126 | convolution fusion | flops 8644444160 | bytes 71401472 | tf_op jit(solution)/shard_map/dot_general | solution.py:47
  706.0 15.5 fusion.168
  721.6 14.7 fusion.169
  749.9 242.9 %all-reduce.7.cloned.1.call-done = (bf16[1024,2048]{1,0:T(8,128)(2,1)}, bf16[1024,2048]{1,0:T(8,128)(2,1)}) async-done(((bf16[1024,2048]{1,0:T(8,128)(2,1)}, bf16[1024,2048]{1,0:T(8,128)(2,1)}), (bf16[1024,2048]{1,0:T(8,128)(2,1)}, bf16[1024,2048]{1,0:T(8,128)(2,1)})) %all-reduce.7.cloned.1.call-update) | async-done | bytes 8388624 | tf_op jit(solution)/shard_map/psum | solution.py:211
  1026.1 14.5 fusion.102
  1040.7 16.0 convolution_add_fusion
  1057.4 15.9 fusion.160
  1073.3 17.9 convolution_add_fusion.2
  1091.5 15.4 fusion.134
  1106.9 17.1 convolution_add_fusion.1
  1132.5 74.2 %reduce-scatter.22.cloned.1.call-done = f32[64,5]{1,0:T(8,128)} async-done(((f32[2048,5]{1,0:T(8,128)}), f32[64,5]{1,0:T(8,128)}) %reduce-scatter.22.cloned.1.call-update) | async-done | bytes 1296
  1210.3 557.9 %all-reduce.5.cloned.1.call-done = (f32[1024,2048]{1,0:T(8,128)}, f32[1024,2048]{1,0:T(8,128)}) async-done(((f32[1024,2048]{1,0:T(8,128)}, f32[1024,2048]{1,0:T(8,128)}), (f32[1024,2048]{1,0:T(8,128)}, f32[1024,2048]{1,0:T(8,128)})) %all-reduce.5.cloned.1.call-update) | async-done | bytes 16777232 | tf_op jit(solution)/shard_map/psum | solution.py:145
  1773.5 48.7 %reduce-scatter.16.cloned.1.call-done = f32[512,256]{1,0:T(8,128)} async-done(((f32[512,2048]{1,0:T(8,128)}), f32[512,256]{1,0:T(8,128)}) %reduce-scatter.16.cloned.1.call-update) | async-done | bytes 524304 | tf_op jit(solution)/shard_map/reduce_scatter | solution.py:223
  1822.2 96.4 %reduce-scatter.14.cloned.1.call-done = f32[256,1536]{1,0:T(8,128)} async-done(((f32[2048,1536]{1,0:T(8,128)}), f32[256,1536]{1,0:T(8,128)}) %reduce-scatter.14.cloned.1.call-update) | async-done | bytes 1572880 | tf_op jit(solution)/shard_map/reduce_scatter | solution.py:222
  1918.6 120.2 %reduce-scatter.18.cloned.1.call-done = f32[256,2048]{1,0:T(8,128)} async-done(((f32[2048,2048]{1,0:T(8,128)}), f32[256,2048]{1,0:T(8,128)}) %reduce-scatter.18.cloned.1.call-update) | async-done | bytes 2097168 | tf_op jit(solution)/shard_map/reduce_scatter | solution.py:224
  2038.8 120.2 %reduce-scatter.20.cloned.1.call-done = f32[2048,256]{1,0:T(8,128)} async-done(((f32[2048,2048]{1,0:T(8,128)}), f32[2048,256]{1,0:T(8,128)}) %reduce-scatter.20.cloned.1.call-update) | async-done | bytes 2097168 | tf_op jit(solution)/shard_map/reduce_scatter | solution.py:225
  (417 shorter events, 333.8 us)
Async XLA Ops:
  7.2 304.2 %copy-start = (bf16[512,2048]{1,0:T(8,128)(2,1)S(1)}, bf16[512,2048]{1,0:T(8,128)(2,1)}, u32[]{:S(2)}) copy-start(bf16[512,2048]{1,0:T(8,128)(2,1)} %param.32) | copy-start | bytes 6291460
  7.3 154.7 %all-gather.3.cloned.1.call-start = ((), (), s32[]{:S(2)}) async-start(), calls=%async_computation.7 | async-start | bytes 10485760 | tf_op jit(solution)/shard_map/all_gather | solution.py:76
  8.0 303.4 %all-gather.5.cloned.1.call-start = ((), (), s32[]{:S(2)}) async-start(), calls=%async_computation.8 | async-start | bytes 10485760 | tf_op jit(solution)/shard_map/all_gather | solution.py:77
  8.8 984.1 %all-reduce.7.cloned.1.call-start = ((), (), s32[]{:S(2)}) async-start(), calls=%async_computation.17 | async-start | bytes 16777216 | tf_op jit(solution)/shard_map/psum | solution.py:211
  8.9 178.1 %copy-start.48 = (f32[2048]{0:T(1024)}, f32[2048]{0:T(1024)S(1)}, u32[]{:S(2)}) copy-start(f32[2048]{0:T(1024)S(1)} %convert_element_type.255) | copy-start | bytes 24580
  8.9 178.1 %copy-start.50 = (f32[2048]{0:T(1024)}, f32[2048]{0:T(1024)S(1)}, u32[]{:S(2)}) copy-start(f32[2048]{0:T(1024)S(1)} %convert_element_type.256) | copy-start | bytes 24580
  10.2 203.0 %copy-start.33 = (f32[1024,32]{0,1:T(8,128)}, f32[1024,32]{0,1:T(8,128)S(1)}, u32[]{:S(2)}) copy-start(f32[1024,32]{0,1:T(8,128)S(1)} %get-tuple-element.592) | copy-start | bytes 393220
  166.3 20.8 copy-start.40
  254.0 63.0 %copy-start.22 = (bf16[2,512,2,256]{3,2,1,0:T(2,128)(2,1)}, bf16[2,512,2,256]{3,2,1,0:T(2,128)(2,1)S(1)}, u32[]{:S(2)}) copy-start(bf16[2,512,2,256]{3,2,1,0:T(2,128)(2,1)S(1)} %get-tuple-element.219) | copy-start | bytes 3145732
  534.3 11.9 copy-start.25
  534.3 22.9 %slice-start = ((s8[8388608]{0:T(1024)(128)(4,1)}), s8[4194304]{0:T(1024)(128)(4,1)S(1)}, s32[]{:S(2)}) async-start(s8[8388608]{0:T(1024)(128)(4,1)} %bitcast.368), calls=%async_computation.18 | async-start | bytes 8388608
  534.3 22.9 %slice-start.4 = ((s8[8388608]{0:T(1024)(128)(4,1)}), s8[4194304]{0:T(1024)(128)(4,1)S(1)}, s32[]{:S(2)}) async-start(s8[8388608]{0:T(1024)(128)(4,1)} %bitcast.408), calls=%async_computation.22 | async-start | bytes 8388608
  557.3 11.9 copy-start.44
  557.3 11.9 copy-start.52
  557.3 11.9 copy-start.57
  638.7 14.8 copy-start.71
  653.5 20.4 copy-start.42
  653.5 20.4 copy-start.49
  653.5 20.4 copy-start.55
  703.6 421.1 %reduce-scatter.24.cloned.1.call-start = ((), (), s32[]{:S(2)}) async-start(), calls=%async_computation.14 | async-start | bytes 442368
  721.5 404.7 %reduce-scatter.26.cloned.1.call-start = ((), (), s32[]{:S(2)}) async-start(), calls=%async_computation.15 | async-start | bytes 1179648
  721.6 17.3 copy-start.23
  740.5 466.3 %reduce-scatter.22.cloned.1.call-start = ((), (), s32[]{:S(2)}) async-start(), calls=%async_computation.13 | async-start | bytes 1081344
  1004.4 763.8 %all-reduce.5.cloned.1.call-start = ((), (), s32[]{:S(2)}) async-start(), calls=%async_computation.16 | async-start | bytes 33554432 | tf_op jit(solution)/shard_map/psum | solution.py:145
  1014.0 808.2 %reduce-scatter.16.cloned.1.call-start = ((), (), s32[]{:S(2)}) async-start(), calls=%async_computation.10 | async-start | bytes 4718592 | tf_op jit(solution)/shard_map/reduce_scatter | solution.py:223
  1025.5 893.1 %reduce-scatter.14.cloned.1.call-start = ((), (), s32[]{:S(2)}) async-start(), calls=%async_computation.9 | async-start | bytes 14155776 | tf_op jit(solution)/shard_map/reduce_scatter | solution.py:222
  1026.1 14.5 copy-start.26
  1056.7 982.0 %reduce-scatter.18.cloned.1.call-start = ((), (), s32[]{:S(2)}) async-start(), calls=%async_computation.11 | async-start | bytes 18874368 | tf_op jit(solution)/shard_map/reduce_scatter | solution.py:224
  1057.4 15.9 copy-start.70
  1091.2 1067.7 %reduce-scatter.20.cloned.1.call-start = ((), (), s32[]{:S(2)}) async-start(), calls=%async_computation.12 | async-start | bytes 18874368 | tf_op jit(solution)/shard_map/reduce_scatter | solution.py:225
  1091.5 15.4 copy-start.69
  1207.9 951.0 %copy-start.67 = (f32[1,64]{1,0:T(1,128)}, f32[1,64]{1,0:T(1,128)S(1)}, u32[]{:S(2)}) copy-start(f32[1,64]{1,0:T(1,128)S(1)} %copy.159) | copy-start | bytes 772
  (73 other events, 316.3 us)
Sparse Core Ops, SparseCore 0:
  9.6 152.3 all-gather.2
  163.6 147.7 all-gather.4
  703.8 289.0 all-reduce.6
  995.7 32.8 reduce-scatter.23
  1031.7 35.9 reduce-scatter.25
  1069.8 136.9 reduce-scatter.21
  1209.4 558.7 all-reduce.4
  1772.1 49.9 reduce-scatter.15
  1826.2 92.3 reduce-scatter.13
  1922.6 116.1 reduce-scatter.17
  2042.9 115.9 reduce-scatter.19
where the time goes:
time: 2180 us; the launch traced here: 2170 us
  waiting for transfers between devices  1470 us (67%)
  matrix products  433 us (20%)
  local copies, waits for them, and re-layouts  175 us (8%)
  other arithmetic  70 us (3%)
    psum x1, waiting for transfers between devices, local(): summed = lax.psum(partial_out, 'tensor')  558 us
    psum x1, waiting for transfers between devices, local(): lax.psum(normed_grad.astype(jnp.bfloat16), 'tensor').astype(jnp.float32)  243 us
    all_gather x1, waiting for transfers between devices, local(): lax.all_gather(hidden_in, 'tensor', axis=1, tiled=True)  148 us
    reduce_scatter x1, waiting for transfers between devices, local(): lax.psum_scatter(up_acc, 'dp', scatter_dimension=0, tiled=True)  120 us
    reduce_scatter x1, waiting for transfers between devices, local(): lax.psum_scatter(down_acc, 'dp', scatter_dimension=1, tiled=True)  120 us
    dot_general x8, matrix products, contract_cols(): lax.dot_general(left, right, (((1,), (1,)), ((), ())), preferred_element_...  118 us
    dot_general x8, matrix products, contract_rows(): lax.dot_general(left, right, (((0,), (0,)), ((), ())), preferred_element_...  108 us
    reduce_scatter x1, waiting for transfers between devices, local(): lax.psum_scatter(qkv_acc, 'dp', scatter_dimension=0, tiled=True)  96.4 us
  transfers between devices with their start and end apart: 11, of which 9 were waited for; matrix products, arithmetic and copies ran while one was open for 13% of the time, Pallas kernels for 0%

commit v1 on v0

v1 whole, which is shorter than its diff:
```python
import math

import jax
import jax.numpy as jnp
from jax import lax
from jax.sharding import PartitionSpec as P

ROT = 64


layer_eps = 1e-05
rope_base = 10000.0
mask_fill = -1e30


def rope_tables(length, rot_dims):
    half = rot_dims // 2
    freqs = jnp.exp(-jnp.log(rope_base) * (2.0 * jnp.arange(half, dtype=jnp.float32) / rot_dims))
    angles = jnp.arange(length, dtype=jnp.float32)[:, None] * freqs[None, :]
    return (jnp.cos(angles), jnp.sin(angles))


def rotate(field, cosine, sine, rot_dims, sign):
    half = rot_dims // 2
    first = field[..., :half]
    second = field[..., half:rot_dims]
    rest = field[..., rot_dims:]
    cos_b = cosine[None, :, None, :]
    sin_b = sign * sine[None, :, None, :]
    return jnp.concatenate(
        [first * cos_b - second * sin_b, second * cos_b + first * sin_b, rest], axis=-1
    )


def gelu_exact(field):
    return jax.nn.gelu(field, approximate=False)


def mm(left, right, dims):
    return lax.dot_general(left, right, (dims, ((), ())), preferred_element_type=jnp.float32)


def local(
    hidden_in,
    keep_slot,
    out_grad,
    ln1_gain,
    ln1_bias,
    ln2_gain,
    ln2_bias,
    qkv_weight,
    qkv_bias,
    dense_weight,
    dense_bias,
    fc1_weight,
    fc1_bias,
    fc2_weight,
    fc2_bias,
):
    slots, own_len, width = hidden_in.shape
    seq_len = own_len * lax.axis_size("tensor")
    head_local, three_hd = qkv_bias.shape
    head_dim = three_hd // 3
    ff_local = fc1_weight.shape[1]
    scale = 1.0 / math.sqrt(head_dim)
    keep = keep_slot.astype(jnp.float32)[:, None, None]

    inputs_all = lax.all_gather(hidden_in, "tensor", axis=1, tiled=True)
    grads_all = lax.all_gather(out_grad, "tensor", axis=1, tiled=True)
    cosine, sine = rope_tables(seq_len, ROT)

    rows = inputs_all.astype(jnp.float32)
    centred = rows - jnp.mean(rows, axis=-1, keepdims=True)
    inv_std = lax.rsqrt(jnp.mean(centred * centred, axis=-1, keepdims=True) + layer_eps)
    normed = centred * inv_std
    g1 = ln1_gain.astype(jnp.float32)
    g2 = ln2_gain.astype(jnp.float32)
    normed_one = (normed * g1 + ln1_bias.astype(jnp.float32)).astype(jnp.bfloat16)
    normed_two = (normed * g2 + ln2_bias.astype(jnp.float32)).astype(jnp.bfloat16)

    joined = mm(normed_one, qkv_weight, ((2,), (0,))) + qkv_bias.reshape(-1).astype(jnp.float32)
    joined = joined.reshape(slots, seq_len, head_local, 3, head_dim)
    query_rot = rotate(joined[:, :, :, 0], cosine, sine, ROT, 1.0).astype(jnp.bfloat16)
    key_rot = rotate(joined[:, :, :, 1], cosine, sine, ROT, 1.0).astype(jnp.bfloat16)
    value_rows = joined[:, :, :, 2].astype(jnp.bfloat16)

    pos = jnp.arange(seq_len)
    allowed = (pos[None, :] <= pos[:, None])[None, None]
    scores = jnp.einsum(
        "sqhd,skhd->shqk", query_rot, key_rot, preferred_element_type=jnp.float32
    ) * scale
    scores = jnp.where(allowed, scores, mask_fill)
    top = jnp.max(scores, axis=-1, keepdims=True)
    weights = jnp.exp(scores - top)
    total = jnp.sum(weights, axis=-1, keepdims=True)
    probs = weights / total
    probs_low = probs.astype(jnp.bfloat16)
    mixed = jnp.einsum(
        "shqk,skhd->sqhd", probs_low, value_rows, preferred_element_type=jnp.float32
    )
    attn_rows = mixed.astype(jnp.bfloat16).reshape(slots, seq_len, head_local * head_dim)

    pre_act = mm(normed_two, fc1_weight, ((2,), (0,))) + fc1_bias.astype(jnp.float32)
    act_val, act_back = jax.vjp(gelu_exact, pre_act)
    act_low = act_val.astype(jnp.bfloat16)
    partial_out = mm(attn_rows, dense_weight, ((2,), (0,))) + mm(act_low, fc2_weight, ((2,), (0,)))
    branch_own = lax.psum_scatter(partial_out, "tensor", scatter_dimension=1, tiled=True)
    branch_own = branch_own + dense_bias.astype(jnp.float32) + fc2_bias.astype(jnp.float32)
    own_in = hidden_in.astype(jnp.float32)
    block_out = (own_in + keep * branch_own).astype(jnp.bfloat16)

    keep_low = keep_slot.astype(jnp.bfloat16)[:, None, None]
    branch_grad = grads_all * keep_low
    own_cot = out_grad.astype(jnp.float32)
    out_bias_part = jnp.sum(own_cot * keep, axis=(0, 1))

    down_grad = mm(act_low, branch_grad, ((0, 1), (0, 1)))
    dense_grad = mm(attn_rows, branch_grad, ((0, 1), (0, 1)))
    act_grad = mm(branch_grad, fc2_weight, ((2,), (1,)))
    pre_grad = act_back(act_grad)[0].astype(jnp.bfloat16)
    up_bias_grad = jnp.sum(pre_grad.astype(jnp.float32), axis=(0, 1))
    up_grad = mm(normed_two, pre_grad, ((0, 1), (0, 1)))
    normed_two_grad = mm(pre_grad, fc1_weight, ((2,), (1,)))
    mixed_grad = mm(branch_grad, dense_weight, ((2,), (1,))).astype(jnp.bfloat16)
    mixed_grad = mixed_grad.reshape(slots, seq_len, head_local, head_dim)

    prob_grad = jnp.einsum(
        "sqhd,skhd->shqk", mixed_grad, value_rows, preferred_element_type=jnp.float32
    )
    inner = jnp.sum(probs * prob_grad, axis=-1, keepdims=True)
    score_grad = (probs * (prob_grad - inner)).astype(jnp.bfloat16)
    query_grad = jnp.einsum(
        "shqk,skhd->sqhd", score_grad, key_rot, preferred_element_type=jnp.float32
    ) * scale
    key_grad = jnp.einsum(
        "shqk,sqhd->skhd", score_grad, query_rot, preferred_element_type=jnp.float32
    ) * scale
    value_grad = jnp.einsum(
        "shqk,sqhd->skhd", probs_low, mixed_grad, preferred_element_type=jnp.float32
    )
    query_grad = rotate(query_grad, cosine, sine, ROT, -1.0)
    key_grad = rotate(key_grad, cosine, sine, ROT, -1.0)
    joined_grad = (
        jnp.stack([query_grad, key_grad, value_grad], axis=3)
        .reshape(slots, seq_len, head_local * three_hd)
        .astype(jnp.bfloat16)
    )
    qkv_bias_grad = jnp.sum(joined_grad.astype(jnp.float32), axis=(0, 1))
    qkv_grad = mm(normed_one, joined_grad, ((0, 1), (0, 1)))
    normed_one_grad = mm(joined_grad, qkv_weight, ((2,), (1,)))

    gain_one = jnp.sum(normed_one_grad * normed, axis=(0, 1))
    shift_one = jnp.sum(normed_one_grad, axis=(0, 1))
    gain_two = jnp.sum(normed_two_grad * normed, axis=(0, 1))
    shift_two = jnp.sum(normed_two_grad, axis=(0, 1))
    normed_grad = normed_one_grad * g1 + normed_two_grad * g2
    own_grad = lax.psum_scatter(
        normed_grad.astype(jnp.bfloat16), "tensor", scatter_dimension=1, tiled=True
    ).astype(jnp.float32)

    own_c = own_in - jnp.mean(own_in, axis=-1, keepdims=True)
    own_inv = lax.rsqrt(jnp.mean(own_c * own_c, axis=-1, keepdims=True) + layer_eps)
    own_normed = own_c * own_inv
    back_rows = own_inv * (
        own_grad
        - jnp.mean(own_grad, axis=-1, keepdims=True)
        - own_normed * jnp.mean(own_grad * own_normed, axis=-1, keepdims=True)
    )
    hidden_grad = own_cot + back_rows

    weight_parts = (
        lax.psum_scatter(qkv_grad, "dp", scatter_dimension=0, tiled=True),
        lax.psum_scatter(dense_grad, "dp", scatter_dimension=1, tiled=True),
        lax.psum_scatter(up_grad, "dp", scatter_dimension=0, tiled=True),
        lax.psum_scatter(down_grad, "dp", scatter_dimension=1, tiled=True),
        lax.psum_scatter(
            qkv_bias_grad.reshape(head_local, three_hd), "dp", scatter_dimension=1, tiled=True
        ),
        lax.psum_scatter(up_bias_grad.reshape(1, -1), "dp", scatter_dimension=1, tiled=True),
    )
    small_parts = lax.psum_scatter(
        jnp.stack([gain_one, shift_one, gain_two, shift_two, out_bias_part]),
        ("dp", "tensor"),
        scatter_dimension=1,
        tiled=True,
    )
    return (
        block_out,
        hidden_grad,
        small_parts[0],
        small_parts[1],
        small_parts[2],
        small_parts[3],
        weight_parts[0],
        weight_parts[4],
        weight_parts[1],
        small_parts[4],
        weight_parts[2],
        weight_parts[5],
        weight_parts[3],
        small_parts[4],
    )


def solution(mesh):
    in_specs = (
        P("dp", "tensor", None),
        P("dp"),
        P("dp", "tensor", None),
        P(),
        P(),
        P(),
        P(),
        P(None, "tensor"),
        P("tensor", None),
        P("tensor", None),
        P(),
        P(None, "tensor"),
        P("tensor"),
        P("tensor", None),
        P(),
    )
    out_specs = (
        P("dp", "tensor", None),
        P("dp", "tensor", None),
        P(("dp", "tensor")),
        P(("dp", "tensor")),
        P(("dp", "tensor")),
        P(("dp", "tensor")),
        P("dp", "tensor"),
        P("tensor", "dp"),
        P("tensor", "dp"),
        P(("dp", "tensor")),
        P("dp", "tensor"),
        P("tensor", "dp"),
        P("tensor", "dp"),
        P(("dp", "tensor")),
    )
    return jax.shard_map(local, mesh=mesh, in_specs=in_specs, out_specs=out_specs, check_vma=False)
```

time: 2180 us -> 1590 us (0.73)
  waiting for transfers between devices: 1470 us -> 1080 us
  matrix products: 433 us -> 313 us
  local copies, waits for them, and re-layouts: 175 us -> 67.8 us
  other arithmetic: 70 us -> 104 us
    psum x2 -> x0, waiting for transfers between devices: 801 us -> none  [the longest x1 558 us: local(): summed = lax.psum(partial_out, 'tensor')]
    reduce_scatter x4 -> x6, waiting for transfers between devices: 385 us -> 755 us  [the longest x1 280 us: local(): lax.psum_scatter(partial_out, 'tensor', scatter_dimension=1, tiled=True)]
    dot_general x52 -> x17, matrix products: 433 us -> 299 us  [the longest x12 256 us: mm(): lax.dot_general(left, right, (dims, ((), ())), preferred_element_type=jnp...]
    convert_element_type x11 -> x10, other arithmetic: 8.84 us -> 60.8 us  [the longest x1 41.4 us: local(): act_low = act_val.astype(jnp.bfloat16)]
    dynamic_update_slice x8 -> x0, local copies, waits for them, and re-layouts: 50.1 us -> none  [the longest x4 46.2 us: local(): lax.scan(attend_back, (empty, empty), (query_blocks, grad_blocks, log_tot...]
    unnamed x14, waiting for transfers between devices: 75.8 us -> 121 us
  transfers between devices with their start and end apart: 11 -> 11, of which waited for: 9 -> 9; matrix products, arithmetic and copies ran while one was open for 13% -> 16% of each run, Pallas kernels for 0% -> 0%
where the time goes in v1:
time: 1590 us; the launch traced here: 1580 us
  waiting for transfers between devices  1080 us (68%)
  matrix products  313 us (20%)
  other arithmetic  104 us (7%)
  local copies, waits for them, and re-layouts  67.8 us (4%)
    reduce_scatter x1, waiting for transfers between devices, local(): lax.psum_scatter(partial_out, 'tensor', scatter_dimension=1, tiled=True)  280 us
    dot_general x12, matrix products, mm(): lax.dot_general(left, right, (dims, ((), ())), preferred_element_type=jnp...  256 us
    all_gather x1, waiting for transfers between devices, local(): inputs_all = lax.all_gather(hidden_in, 'tensor', axis=1, tiled=True)  142 us
    unnamed x14, waiting for transfers between devices  121 us
    reduce_scatter x1, waiting for transfers between devices, local(): lax.psum_scatter(up_grad, 'dp', scatter_dimension=0, tiled=True)  120 us
    reduce_scatter x1, waiting for transfers between devices, local(): lax.psum_scatter(down_grad, 'dp', scatter_dimension=1, tiled=True)  120 us
    reduce_scatter x1, waiting for transfers between devices, local(): lax.psum_scatter(qkv_grad, 'dp', scatter_dimension=0, tiled=True)  96.4 us
    reduce_scatter x1, waiting for transfers between devices, local(): lax.psum_scatter(normed_grad.astype(jnp.bfloat16), 'tensor', scatter_dime...  90.7 us
  transfers between devices with their start and end apart: 11, of which 9 were waited for; matrix products, arithmetic and copies ran while one was open for 16% of the time, Pallas kernels for 0%

profile of v1, /device:TPU:0, one launch (start us, length us, event | category | flops | bytes accessed | tf_op | source)
XLA Modules:
  0.0 1582.1 jit_solution(7778347969194694805)
XLA Ops:
  19.9 142.1 %all-gather.3.cloned.1.call-done = bf16[2,1024,2048]{2,1,0:T(8,128)(2,1)} async-done(((bf16[2,256,2048]{2,1,0:T(8,128)(2,1)}), bf16[2,1024,2048]{2,1,0:T(8,128)(2,1)}) %all-gather.3.cloned.1.call-update) | async-done | bytes 8388624 | tf_op jit(solution)/shard_map/all_gather | solution.py:68
  170.7 16.2 %convolution_add_fusion = f32[2,1024,1536]{2,1,0:T(8,128)} fusion(bf16[2048,1536]{1,0:T(8,128)(2,1)S(1)} %copy-done.28, f32[1536]{0:T(1024)S(1)} %reshape.182, bf16[2,1024,2048]{2,1,0:T(8,128)(2,1)S(1)} %copy-done.1, f32[2048]{0:T(1024)S(1)} %convert_element_type.106, f32[2048]{0:T(1024)S(1)} %convert_element_type.105, f32[2,1024]{1,0:T(2,128)S(1)} %add_rsqrt_fusion, ...), kind=kOutput, calls=%fused_computation.61 | convolution fusion | flops 12913213440 | bytes 27301888 | tf_op jit(solution)/shard_map/dot_general | solution.py:40
  186.9 12.6 copy.69
  199.5 8.5 fusion.96
  234.7 14.7 fusion.99
  249.4 62.0 %all-gather.5.cloned.1.call-done = bf16[2,1024,2048]{2,1,0:T(8,128)(2,1)} async-done(((bf16[2,256,2048]{2,1,0:T(8,128)(2,1)}), bf16[2,1024,2048]{2,1,0:T(8,128)(2,1)}) %all-gather.5.cloned.1.call-update) | async-done | bytes 8388624 | tf_op jit(solution)/shard_map/all_gather | solution.py:69
  311.3 8.3 fusion.79
  319.6 9.5 fusion.69
  329.1 11.8 multiply_reduce_fusion
  341.0 13.0 multiply_convert_fusion
  359.9 8.5 multiply_bitcast_fusion.1
  379.6 8.7 copy.85
  388.3 20.7 %fusion.34 = f32[2,1024,2048]{2,1,0:T(8,128)} fusion(bf16[2,1024,1536]{1,2,0:T(8,128)(2,1)} %bitcast.101, bf16[2048,1536]{1,0:T(8,128)(2,1)} %param.22), kind=kOutput, calls=%fused_computation.62 | convolution fusion | flops 12884901888 | bytes 29360128 | tf_op jit(solution)/shard_map/dot_general | solution.py:40
  409.0 30.9 %fusion.65 = (u8[1024,2048]{1,0:T(8,128)(4,1)S(1)}, u8[1024,2048]{1,0:T(8,128)(4,1)S(1)}, f32[2,1024,2048]{2,1,0:T(8,128)}) fusion(f32[2048]{0:T(1024)S(1)} %copy-done.8, bf16[2048,2048]{1,0:T(8,128)(2,1)} %param.26, bf16[2,1024,2048]{2,1,0:T(8,128)(2,1)} %all-gather.3.cloned.1.call-done, f32[2048]{0:T(1024)S(1)} %copy-done.16, f32[2048]{0:T(1024)S(1)} %copy-done.14, ...), kind=kOutput, calls=%fused_computation.105 | convolution fusion | flops 17259560960 | bytes 37789696 | tf_op jit(solution)/shard_map/dot_general | solution.py:40
  439.9 41.4 %multiply_convert_fusion.1 = (bf16[2,1024,2048]{2,1,0:T(8,128)(2,1)}, f32[2,1024,2048]{2,1,0:T(8,128)}) fusion(f32[2,1024,2048]{2,1,0:T(8,128)} %get-tuple-element.56, f32[2048]{0:T(1024)S(1)} %copy-done.8, u8[1024,2048]{1,0:T(8,128)(4,1)S(1)} %get-tuple-element.15, u8[1024,2048]{1,0:T(8,128)(4,1)S(1)} %get-tuple-element.14), kind=kLoop, calls=%fused_computation.28 | loop fusion | flops 297795584 | bytes 46145536 | tf_op jit(solution)/shard_map/convert_element_type | solution.py:105
  481.3 31.6 %convert_reduce_fusion.1 = (f32[2048]{0:T(1024)S(1)}, bf16[2,1024,2048]{2,1,0:T(8,128)(2,1)}) fusion(f32[2,1024,2048]{2,1,0:T(8,128)} %get-tuple-element.25, bf16[2048,2048]{1,0:T(8,128)(2,1)} %param.28, bf16[2,1024,2048]{2,1,0:T(8,128)(2,1)} %all-gather.5.cloned.1.call-done, bf16[2]{0:T(256)(128)(2,1)S(1)} %copy-done.31, ...), kind=kOutput, calls=%fused_computation.23 | convolution fusion | flops 17255364608 | bytes 58736644 | tf_op jit(solution)/shard_map/dot_general | solution.py:40
  512.8 31.3 %fusion.93 = (f32[2048]{0:T(1024)S(1)}, f32[2048]{0:T(1024)S(1)}, bf16[2,1024,2048]{2,1,0:T(8,128)(2,1)}, f32[2048]{0:T(1024)S(1)}, f32[2048]{0:T(1024)S(1)}) fusion(f32[2,1024]{1,0:T(2,128)S(1)} %copy-done.23, f32[2,1024]{1,0:T(2,128)S(1)} %copy-done.10, bf16[2,1024,2048]{2,1,0:T(8,128)(2,1)} %all-gather.3.cloned.1.call-done, f32[2048]{0:T(1024)S(1)} %copy-done.14, ...), kind=kOutput, calls=%fused_computation.139 | convolution fusion | flops 17234386944 | bytes 50397184 | tf_op jit(solution)/shard_map/dot_general | solution.py:40
  544.9 10.2 fusion.76
  555.1 8.2 fusion.74
  563.3 26.3 %fusion.31 = f32[2,1024,2048]{2,1,0:T(8,128)} fusion(f32[2,1024,2048]{2,1,0:T(8,128)} %fusion.74, bf16[2,1024,2048]{2,1,0:T(8,128)(2,1)} %get-tuple-element.24, bf16[2048,2048]{1,0:T(8,128)(2,1)} %param.28), kind=kOutput, calls=%fused_computation.60 | convolution fusion | flops 17184063488 | bytes 50331648 | tf_op jit(solution)/shard_map/dot_general | solution.py:40
  596.4 90.7 %reduce-scatter.18.cloned.1.call-done = bf16[2,256,2048]{2,1,0:T(8,128)(2,1)} async-done(((bf16[2,1024,2048]{2,1,0:T(8,128)(2,1)}), bf16[2,256,2048]{2,1,0:T(8,128)(2,1)}) %reduce-scatter.18.cloned.1.call-update) | async-done | bytes 2097168 | tf_op jit(solution)/shard_map/reduce_scatter | solution.py:157
  690.9 279.6 %reduce-scatter.16.cloned.1.call-done = f32[2,256,2048]{2,1,0:T(8,128)} async-done(((f32[2,1024,2048]{2,1,0:T(8,128)}), f32[2,256,2048]{2,1,0:T(8,128)}) %reduce-scatter.16.cloned.1.call-update) | async-done | bytes 4194320 | tf_op jit(solution)/shard_map/reduce_scatter | solution.py:107
  970.5 7.7 fusion.53
  979.7 10.7 fusion.66
  990.6 22.1 %convolution_bitcast_fusion = f32[2048,1536]{1,0:T(8,128)} fusion(bf16[2,1024,1536]{1,2,0:T(8,128)(2,1)} %bitcast.102, bf16[2,1024,2048]{2,1,0:T(8,128)(2,1)} %all-gather.3.cloned.1.call-done, f32[2048]{0:T(1024)S(1)} %copy-done.21, f32[2048]{0:T(1024)S(1)} %copy-done.19, f32[2,1024]{1,0:T(2,128)S(1)} %copy-done.23, f32[2,1024]{1,0:T(2,128)S(1)} %copy-done.10), kind=kOutput, calls=%fused_computation.46 | convolution fusion | flops 12910067712 | bytes 27295744 | tf_op jit(solution)/shard_map/dot_general | solution.py:40
  1012.8 24.7 %convolution_bitcast_fusion.1 = f32[2048,2048]{1,0:T(8,128)} fusion(bf16[2,1024,2048]{2,1,0:T(8,128)(2,1)} %get-tuple-element.24, bf16[2,1024,2048]{2,1,0:T(8,128)(2,1)} %all-gather.5.cloned.1.call-done, bf16[2]{0:T(256)(128)(2,1)S(1)} %copy-done.31), kind=kOutput, calls=%fused_computation.47 | convolution fusion | flops 17184063488 | bytes 33554436 | tf_op jit(solution)/shard_map/dot_general | solution.py:40
  1038.2 25.1 %convolution_bitcast_fusion.2 = f32[2048,2048]{1,0:T(8,128)} fusion(bf16[2,1024,2048]{2,1,0:T(8,128)(2,1)} %get-tuple-element.62, bf16[2,1024,2048]{2,1,0:T(8,128)(2,1)} %all-gather.3.cloned.1.call-done, f32[2048]{0:T(1024)S(1)} %copy-done.17, f32[2048]{0:T(1024)S(1)} %copy-done.15, f32[2,1024]{1,0:T(2,128)S(1)} %copy-done.23, f32[2,1024]{1,0:T(2,128)S(1)} %copy-done.10), kind=kOutput, calls=%fused_computation.48 | convolution fusion | flops 17205035008 | bytes 33587200 | tf_op jit(solution)/shard_map/dot_general | solution.py:40
  1066.3 119.9 %reduce-scatter.28.cloned.1.call-done = f32[64,5]{1,0:T(8,128)} async-done(((f32[2048,5]{1,0:T(8,128)}), f32[64,5]{1,0:T(8,128)}) %reduce-scatter.28.cloned.1.call-update) | async-done | bytes 1296
  1189.7 48.4 %reduce-scatter.22.cloned.1.call-done = f32[512,256]{1,0:T(8,128)} async-done(((f32[512,2048]{1,0:T(8,128)}), f32[512,256]{1,0:T(8,128)}) %reduce-scatter.22.cloned.1.call-update) | async-done | bytes 524304 | tf_op jit(solution)/shard_map/reduce_scatter | solution.py:173
  1238.1 96.4 %reduce-scatter.20.cloned.1.call-done = f32[256,1536]{1,0:T(8,128)} async-done(((f32[2048,1536]{1,0:T(8,128)}), f32[256,1536]{1,0:T(8,128)}) %reduce-scatter.20.cloned.1.call-update) | async-done | bytes 1572880 | tf_op jit(solution)/shard_map/reduce_scatter | solution.py:172
  1334.5 120.0 %reduce-scatter.26.cloned.1.call-done = f32[2048,256]{1,0:T(8,128)} async-done(((f32[2048,2048]{1,0:T(8,128)}), f32[2048,256]{1,0:T(8,128)}) %reduce-scatter.26.cloned.1.call-update) | async-done | bytes 2097168 | tf_op jit(solution)/shard_map/reduce_scatter | solution.py:175
  1454.5 120.4 %reduce-scatter.24.cloned.1.call-done = f32[256,2048]{1,0:T(8,128)} async-done(((f32[2048,2048]{1,0:T(8,128)}), f32[256,2048]{1,0:T(8,128)}) %reduce-scatter.24.cloned.1.call-update) | async-done | bytes 2097168 | tf_op jit(solution)/shard_map/reduce_scatter | solution.py:174
  (135 shorter events, 85.7 us)
Async XLA Ops:
  7.2 304.2 %copy-start = (bf16[512,2048]{1,0:T(8,128)(2,1)S(1)}, bf16[512,2048]{1,0:T(8,128)(2,1)}, u32[]{:S(2)}) copy-start(bf16[512,2048]{1,0:T(8,128)(2,1)} %param.24) | copy-start | bytes 6291460
  7.2 154.7 %all-gather.3.cloned.1.call-start = ((), (), s32[]{:S(2)}) async-start(), calls=%async_computation.9 | async-start | bytes 10485760 | tf_op jit(solution)/shard_map/all_gather | solution.py:68
  7.9 303.4 %all-gather.5.cloned.1.call-start = ((), (), s32[]{:S(2)}) async-start(), calls=%async_computation.11 | async-start | bytes 10485760 | tf_op jit(solution)/shard_map/all_gather | solution.py:69
  8.7 678.5 %reduce-scatter.18.cloned.1.call-start = ((), (), s32[]{:S(2)}) async-start(), calls=%async_computation.12 | async-start | bytes 10485760 | tf_op jit(solution)/shard_map/reduce_scatter | solution.py:157
  9.4 160.7 %copy-start.18 = (f32[2048]{0:T(1024)}, f32[2048]{0:T(1024)S(1)}, u32[]{:S(2)}) copy-start(f32[2048]{0:T(1024)S(1)} %convert_element_type.105) | copy-start | bytes 24580
  12.7 157.4 %copy-start.20 = (f32[2048]{0:T(1024)}, f32[2048]{0:T(1024)S(1)}, u32[]{:S(2)}) copy-start(f32[2048]{0:T(1024)S(1)} %convert_element_type.106) | copy-start | bytes 24580
  17.2 294.2 %copy-start.30 = (bf16[2]{0:T(256)(128)(2,1)}, bf16[2]{0:T(256)(128)(2,1)S(1)}, u32[]{:S(2)}) copy-start(bf16[2]{0:T(256)(128)(2,1)S(1)} %get-tuple-element.54) | copy-start | bytes 16
  161.9 5.8 copy-start.1
  161.9 8.7 copy-start.28
  249.3 91.6 %copy-start.12 = (f32[2,2,1024]{2,1,0:T(2,128)}, f32[2,2,1024]{2,1,0:T(2,128)S(1)}, u32[]{:S(2)}) copy-start(f32[2,2,1024]{2,1,0:T(2,128)S(1)} %get-tuple-element.57) | copy-start | bytes 49156
  341.0 16.2 %copy-start.4 = (bf16[2,1024,2,192]{3,1,2,0:T(8,128)(2,1)S(1)}, bf16[2,1024,2,192]{3,1,2,0:T(8,128)(2,1)}, u32[]{:S(2)}) copy-start(bf16[2,1024,2,192]{3,1,2,0:T(8,128)(2,1)} %slice.123) | copy-start | bytes 4718596
  341.0 16.2 %copy-start.6 = (bf16[2,1024,2,32]{3,1,2,0:T(8,128)(2,1)S(1)}, bf16[2,1024,2,32]{3,1,2,0:T(8,128)(2,1)}, u32[]{:S(2)}) copy-start(bf16[2,1024,2,32]{3,1,2,0:T(8,128)(2,1)} %get-tuple-element.35) | copy-start | bytes 786436
  341.0 16.2 %copy-start.7 = (bf16[2,1024,2,32]{3,1,2,0:T(8,128)(2,1)S(1)}, bf16[2,1024,2,32]{3,1,2,0:T(8,128)(2,1)}, u32[]{:S(2)}) copy-start(bf16[2,1024,2,32]{3,1,2,0:T(8,128)(2,1)} %get-tuple-element.36) | copy-start | bytes 786436
  388.3 20.7 %copy-start.8 = (f32[2048]{0:T(1024)S(1)}, f32[2048]{0:T(1024)}, u32[]{:S(2)}) copy-start(f32[2048]{0:T(1024)} %convert_element_type.117) | copy-start | bytes 24580
  388.3 20.7 %copy-start.10 = (f32[2,1024]{1,0:T(2,128)S(1)}, f32[2,1024]{1,0:T(2,128)}, u32[]{:S(2)}) copy-start(f32[2,1024]{1,0:T(2,128)} %copy-done.9) | copy-start | bytes 24580
  388.3 20.7 %copy-start.14 = (f32[2048]{0:T(1024)S(1)}, f32[2048]{0:T(1024)}, u32[]{:S(2)}) copy-start(f32[2048]{0:T(1024)} %convert_element_type.114) | copy-start | bytes 24580
  388.3 20.7 %copy-start.16 = (f32[2048]{0:T(1024)S(1)}, f32[2048]{0:T(1024)}, u32[]{:S(2)}) copy-start(f32[2048]{0:T(1024)} %convert_element_type.115) | copy-start | bytes 24580
  388.3 20.7 %copy-start.23 = (f32[2,1024]{1,0:T(2,128)S(1)}, f32[2,1024]{1,0:T(2,128)}, u32[]{:S(2)}) copy-start(f32[2,1024]{1,0:T(2,128)} %copy-done.22) | copy-start | bytes 24580
  439.9 41.4 %copy-start.31 = (bf16[2]{0:T(256)(128)(2,1)S(1)}, bf16[2]{0:T(256)(128)(2,1)}, u32[]{:S(2)}) copy-start(bf16[2]{0:T(256)(128)(2,1)} %copy-done.30) | copy-start | bytes 16
  481.3 31.6 %copy-start.19 = (f32[2048]{0:T(1024)S(1)}, f32[2048]{0:T(1024)}, u32[]{:S(2)}) copy-start(f32[2048]{0:T(1024)} %copy-done.18) | copy-start | bytes 24580
  544.2 426.3 %reduce-scatter.16.cloned.1.call-start = ((), (), s32[]{:S(2)}) async-start(), calls=%async_computation.10 | async-start | bytes 20971520 | tf_op jit(solution)/shard_map/reduce_scatter | solution.py:107
  555.1 8.2 copy-start.29
  589.6 380.9 %copy-start.26 = (f32[2]{0:T(128)S(1)}, f32[2]{0:T(128)}, u32[]{:S(2)}) copy-start(f32[2]{0:T(128)} %get-tuple-element.55) | copy-start | bytes 28
  589.6 473.7 %reduce-scatter.30.cloned.1.call-start = ((), (), s32[]{:S(2)}) async-start(), calls=%async_computation.18 | async-start | bytes 442368
  594.9 469.9 %reduce-scatter.32.cloned.1.call-start = ((), (), s32[]{:S(2)}) async-start(), calls=%async_computation.19 | async-start | bytes 1179648
  596.4 589.8 %reduce-scatter.28.cloned.1.call-start = ((), (), s32[]{:S(2)}) async-start(), calls=%async_computation.17 | async-start | bytes 1081344
  979.6 11.0 copy-start.21
  979.6 258.5 %reduce-scatter.22.cloned.1.call-start = ((), (), s32[]{:S(2)}) async-start(), calls=%async_computation.14 | async-start | bytes 4718592 | tf_op jit(solution)/shard_map/reduce_scatter | solution.py:173
  990.4 344.1 %reduce-scatter.20.cloned.1.call-start = ((), (), s32[]{:S(2)}) async-start(), calls=%async_computation.13 | async-start | bytes 14155776 | tf_op jit(solution)/shard_map/reduce_scatter | solution.py:172
  1012.8 441.7 %reduce-scatter.26.cloned.1.call-start = ((), (), s32[]{:S(2)}) async-start(), calls=%async_computation.16 | async-start | bytes 18874368 | tf_op jit(solution)/shard_map/reduce_scatter | solution.py:175
  1037.5 537.3 %reduce-scatter.24.cloned.1.call-start = ((), (), s32[]{:S(2)}) async-start(), calls=%async_computation.15 | async-start | bytes 18874368 | tf_op jit(solution)/shard_map/reduce_scatter | solution.py:174
  1187.3 388.0 %copy-start.27 = (f32[1,64]{1,0:T(1,128)}, f32[1,64]{1,0:T(1,128)S(1)}, u32[]{:S(2)}) copy-start(f32[1,64]{1,0:T(1,128)S(1)} %copy.120) | copy-start | bytes 772
  (11 other events, 29.7 us)
Sparse Core Ops, SparseCore 0:
  9.6 152.3 all-gather.2
  163.5 147.7 all-gather.4
  544.3 142.8 reduce-scatter.17
  689.4 281.0 reduce-scatter.15
  973.4 34.4 reduce-scatter.29
  1010.9 35.9 reduce-scatter.31
  1049.2 137.0 reduce-scatter.27
  1190.2 47.8 reduce-scatter.21
  1242.2 92.2 reduce-scatter.19
  1338.5 115.9 reduce-scatter.25
  1458.6 116.1 reduce-scatter.23

commit v2 on v1

--- a/solution.py
+++ b/solution.py
@@ -38,6 +38,50 @@
 
 def mm(left, right, dims):
     return lax.dot_general(left, right, (dims, ((), ())), preferred_element_type=jnp.float32)
+
+
+def line_all_gather(x, axis_name):
+    n = lax.axis_size(axis_name)
+    idx = lax.axis_index(axis_name)
+    own = x.shape[1]
+    right, left = x, x
+    rights, lefts = [], []
+    for s in range(1, n):
+        right = lax.ppermute(right, axis_name, [(i, i + 1) for i in range(s - 1, n - 1)])
+        left = lax.ppermute(left, axis_name, [(i, i - 1) for i in range(1, n - s + 1)])
+        rights.append(right)
+        lefts.append(left)
+    rel = jnp.concatenate(rights[::-1] + [x] + lefts, axis=1)
+    return lax.dynamic_slice_in_dim(rel, (n - 1 - idx) * own, n * own, axis=1)
+
+
+def line_reduce_scatter(p, axis_name, send_dtype):
+    n = lax.axis_size(axis_name)
+    idx = lax.axis_index(axis_name)
+    own = p.shape[1] // n
+
+    def chunk(k):
+        k = jnp.clip(k, 0, n - 1)
+        return lax.dynamic_slice_in_dim(p, k * own, own, axis=1).astype(jnp.float32)
+
+    recv_r = None
+    recv_l = None
+    for s in range(1, n):
+        send_r = chunk(idx + n - s)
+        send_l = chunk(idx - n + s)
+        if recv_r is not None:
+            send_r = send_r + recv_r.astype(jnp.float32)
+            send_l = send_l + recv_l.astype(jnp.float32)
+        recv_r = lax.ppermute(
+            send_r.astype(send_dtype), axis_name, [(i, i + 1) for i in range(0, min(s, n - 1))]
+        )
+        recv_l = lax.ppermute(
+            send_l.astype(send_dtype), axis_name, [(i, i - 1) for i in range(max(n - s, 1), n)]
+        )
+    out = chunk(idx)
+    if recv_r is not None:
+        out = out + recv_r.astype(jnp.float32) + recv_l.astype(jnp.float32)
+    return out
 
 
 def local(
@@ -65,8 +109,9 @@
     scale = 1.0 / math.sqrt(head_dim)
     keep = keep_slot.astype(jnp.float32)[:, None, None]
 
-    inputs_all = lax.all_gather(hidden_in, "tensor", axis=1, tiled=True)
-    grads_all = lax.all_gather(out_grad, "tensor", axis=1, tiled=True)
+    inputs_all = line_all_gather(hidden_in, "tensor")
+    inputs_all, out_grad_b = lax.optimization_barrier((inputs_all, out_grad))
+    grads_all = line_all_gather(out_grad_b, "tensor")
     cosine, sine = rope_tables(seq_len, ROT)
 
     rows = inputs_all.astype(jnp.float32)
@@ -104,7 +149,7 @@
     act_val, act_back = jax.vjp(gelu_exact, pre_act)
     act_low = act_val.astype(jnp.bfloat16)
     partial_out = mm(attn_rows, dense_weight, ((2,), (0,))) + mm(act_low, fc2_weight, ((2,), (0,)))
-    branch_own = lax.psum_scatter(partial_out, "tensor", scatter_dimension=1, tiled=True)
+    branch_own = line_reduce_scatter(partial_out, "tensor", jnp.float32)
     branch_own = branch_own + dense_bias.astype(jnp.float32) + fc2_bias.astype(jnp.float32)
     own_in = hidden_in.astype(jnp.float32)
     block_out = (own_in + keep * branch_own).astype(jnp.bfloat16)
@@ -116,10 +161,14 @@
 
     down_grad = mm(act_low, branch_grad, ((0, 1), (0, 1)))
     dense_grad = mm(attn_rows, branch_grad, ((0, 1), (0, 1)))
+    down_grad, dense_grad, branch_grad = lax.optimization_barrier(
+        (down_grad, dense_grad, branch_grad)
+    )
     act_grad = mm(branch_grad, fc2_weight, ((2,), (1,)))
     pre_grad = act_back(act_grad)[0].astype(jnp.bfloat16)
     up_bias_grad = jnp.sum(pre_grad.astype(jnp.float32), axis=(0, 1))
     up_grad = mm(normed_two, pre_grad, ((0, 1), (0, 1)))
+    up_grad, pre_grad = lax.optimization_barrier((up_grad, pre_grad))
     normed_two_grad = mm(pre_grad, fc1_weight, ((2,), (1,)))
     mixed_grad = mm(branch_grad, dense_weight, ((2,), (1,))).astype(jnp.bfloat16)
     mixed_grad = mixed_grad.reshape(slots, seq_len, head_local, head_dim)
@@ -147,6 +196,7 @@
     )
     qkv_bias_grad = jnp.sum(joined_grad.astype(jnp.float32), axis=(0, 1))
     qkv_grad = mm(normed_one, joined_grad, ((0, 1), (0, 1)))
+    qkv_grad, joined_grad = lax.optimization_barrier((qkv_grad, joined_grad))
     normed_one_grad = mm(joined_grad, qkv_weight, ((2,), (1,)))
 
     gain_one = jnp.sum(normed_one_grad * normed, axis=(0, 1))
@@ -154,9 +204,7 @@
     gain_two = jnp.sum(normed_two_grad * normed, axis=(0, 1))
     shift_two = jnp.sum(normed_two_grad, axis=(0, 1))
     normed_grad = normed_one_grad * g1 + normed_two_grad * g2
-    own_grad = lax.psum_scatter(
-        normed_grad.astype(jnp.bfloat16), "tensor", scatter_dimension=1, tiled=True
-    ).astype(jnp.float32)
+    own_grad = line_reduce_scatter(normed_grad, "tensor", jnp.bfloat16)
 
     own_c = own_in - jnp.mean(own_in, axis=-1, keepdims=True)
     own_inv = lax.rsqrt(jnp.mean(own_c * own_c, axis=-1, keepdims=True) + layer_eps)

time: 1590 us -> 1710 us (1.075)
  starting transfers between devices: 1.3 us -> 124 us
  waiting for transfers between devices: 1080 us -> 963 us
  local copies, waits for them, and re-layouts: 67.8 us -> 126 us
  other arithmetic: 104 us -> 157 us
    reduce_scatter x2 -> x0, waiting for transfers between devices: 370 us -> none  [the longest x1 280 us: local(): lax.psum_scatter(partial_out, 'tensor', scatter_dimension=1, tiled=True)]
    ppermute x0 -> x24, waiting for transfers between devices: none -> 358 us  [the longest x6 161 us: line_reduce_scatter(): lax.ppermute(send_r.astype(send_dtype), axis_name, [(i, i + 1) for i in r...]
    all_gather x2 -> x0, waiting for transfers between devices: 204 us -> none  [the longest x1 142 us: local(): inputs_all = lax.all_gather(hidden_in, 'tensor', axis=1, tiled=True)]
    ppermute x0 -> x24, starting transfers between devices: none -> 123 us  [the longest x6 87.6 us: line_reduce_scatter(): lax.ppermute(send_r.astype(send_dtype), axis_name, [(i, i + 1) for i in r...]
    unnamed x14 -> x10, waiting for transfers between devices: 121 us -> 220 us
    unnamed x77 -> x111, local copies, waits for them, and re-layouts: 26.1 us -> 63.1 us
    add x0 -> x4, other arithmetic: none -> 30.3 us  [the longest x2 16.7 us: line_reduce_scatter(): send_r = send_r + recv_r.astype(jnp.float32)]
  transfers between devices with their start and end apart: 11 -> 31, of which waited for: 9 -> 16; matrix products, arithmetic and copies ran while one was open for 16% -> 34% of each run, Pallas kernels for 0% -> 0%
where the time goes in v2:
time: 1710 us; the launch traced here: 1700 us
  waiting for transfers between devices  963 us (56%)
  matrix products  316 us (18%)
  other arithmetic  157 us (9%)
  local copies, waits for them, and re-layouts  126 us (7%)
  starting transfers between devices  124 us (7%)
    dot_general x12, matrix products, mm(): lax.dot_general(left, right, (dims, ((), ())), preferred_element_type=jnp...  257 us
    unnamed x10, waiting for transfers between devices  220 us
    ppermute x6, waiting for transfers between devices, line_reduce_scatter(): lax.ppermute(send_r.astype(send_dtype), axis_name, [(i, i + 1) for i in r...  161 us
    reduce_scatter x1, waiting for transfers between devices, local(): lax.psum_scatter(up_grad, 'dp', scatter_dimension=0, tiled=True)  120 us
    reduce_scatter x1, waiting for transfers between devices, local(): lax.psum_scatter(down_grad, 'dp', scatter_dimension=1, tiled=True)  120 us
    ppermute x6, waiting for transfers between devices, line_all_gather(): lax.ppermute(left, axis_name, [(i, i - 1) for i in range(1, n - s + 1)])  115 us
    reduce_scatter x1, waiting for transfers between devices, local(): lax.psum_scatter(qkv_grad, 'dp', scatter_dimension=0, tiled=True)  96.2 us
    ppermute x6, starting transfers between devices, line_reduce_scatter(): lax.ppermute(send_r.astype(send_dtype), axis_name, [(i, i + 1) for i in r...  87.6 us
  transfers between devices with their start and end apart: 31, of which 16 were waited for; matrix products, arithmetic and copies ran while one was open for 34% of the time, Pallas kernels for 0%

profile of v2, /device:TPU:0, one launch (start us, length us, event | category | flops | bytes accessed | tf_op | source)
XLA Modules:
  0.0 1700.2 jit_solution(13186031769196678406)
XLA Ops:
  13.8 43.8 %collective-permute-done = bf16[2,256,2048]{2,1,0:T(8,128)(2,1)S(1)} collective-permute-done((bf16[2,256,2048]{2,1,0:T(8,128)(2,1)}, bf16[2,256,2048]{2,1,0:T(8,128)(2,1)S(1)}, u32[]{:S(2)}, u32[]{:S(2)}) %collective-permute-start) | collective-permute-done | bytes 2097184 | tf_op jit(solution)/shard_map/ppermute | solution.py:50
  69.3 43.5 %collective-permute-done.4 = bf16[2,256,2048]{2,1,0:T(8,128)(2,1)} collective-permute-done((bf16[2,256,2048]{2,1,0:T(8,128)(2,1)}, bf16[2,256,2048]{2,1,0:T(8,128)(2,1)}, u32[]{:S(2)}, u32[]{:S(2)}) %collective-permute-start.4) | collective-permute-done | bytes 2097184 | tf_op jit(solution)/shard_map/ppermute | solution.py:51
  134.1 26.7 %collective-permute-done.5 = bf16[2,256,2048]{2,1,0:T(8,128)(2,1)S(1)} collective-permute-done((bf16[2,256,2048]{2,1,0:T(8,128)(2,1)}, bf16[2,256,2048]{2,1,0:T(8,128)(2,1)S(1)}, u32[]{:S(2)}, u32[]{:S(2)}) %collective-permute-start.5) | collective-permute-done | bytes 2097184 | tf_op jit(solution)/shard_map/ppermute | solution.py:51
  182.6 16.7 convolution_add_fusion
  199.3 12.6 copy.69
  246.7 14.8 fusion.87
  280.5 30.9 %fusion.56 = (u8[1024,2048]{1,0:T(8,128)(4,1)S(1)}, u8[1024,2048]{1,0:T(8,128)(4,1)S(1)}, f32[2,1024,2048]{2,1,0:T(8,128)}) fusion(f32[2048]{0:T(1024)S(1)} %convert_element_type.147, bf16[2048,2048]{1,0:T(8,128)(2,1)} %param.26, bf16[2,1024,2048]{2,1,0:T(8,128)(2,1)} %constant_dynamic-slice_fusion.2, f32[2048]{0:T(1024)S(1)} %convert_element_type.145, ...), kind=kOutput, calls=%fused_computation.105 | convolution fusion | flops 17259560960 | bytes 37789696 | tf_op jit(solution)/shard_map/dot_general | solution.py:40
  311.4 41.2 %multiply_convert_fusion.1 = (bf16[2,1024,2048]{2,1,0:T(8,128)(2,1)S(1)}, f32[2,1024,2048]{2,1,0:T(8,128)}) fusion(f32[2,1024,2048]{2,1,0:T(8,128)} %get-tuple-element.81, f32[2048]{0:T(1024)S(1)} %convert_element_type.147, u8[1024,2048]{1,0:T(8,128)(4,1)S(1)} %get-tuple-element.33, u8[1024,2048]{1,0:T(8,128)(4,1)S(1)} %get-tuple-element.32), kind=kLoop, calls=%fused_computation.28 | loop fusion | flops 297795584 | bytes 46145536 | tf_op jit(solution)/shard_map/convert_element_type | solution.py:150
  352.6 26.6 %fusion.31 = f32[2,1024,2048]{2,1,0:T(8,128)} fusion(f32[2,1024,2048]{2,1,0:T(8,128)} %fusion.63, bf16[2,1024,2048]{2,1,0:T(8,128)(2,1)S(1)} %get-tuple-element.43, bf16[2048,2048]{1,0:T(8,128)(2,1)} %param.28), kind=kOutput, calls=%fused_computation.61 | convolution fusion | flops 17184063488 | bytes 50331648 | tf_op jit(solution)/shard_map/dot_general | solution.py:40
  383.9 16.4 collective-permute-start.6
  406.1 43.4 %collective-permute-done.16 = bf16[2,256,2048]{2,1,0:T(8,128)(2,1)} collective-permute-done((bf16[2,256,2048]{2,1,0:T(8,128)(2,1)}, bf16[2,256,2048]{2,1,0:T(8,128)(2,1)}, u32[]{:S(2)}, u32[]{:S(2)}) %collective-permute-start.16) | collective-permute-done | bytes 2097184 | tf_op jit(solution)/shard_map/ppermute | solution.py:51
  450.8 34.8 %collective-permute-done.6 = f32[2,256,2048]{2,1,0:T(8,128)} collective-permute-done((f32[2,256,2048]{2,1,0:T(8,128)}, f32[2,256,2048]{2,1,0:T(8,128)}, u32[]{:S(2)}, u32[]{:S(2)}) %collective-permute-start.6) | collective-permute-done | bytes 4194336 | tf_op jit(solution)/shard_map/ppermute | solution.py:75
  529.4 24.4 %convolution_bitcast_fusion.2 = f32[2048,2048]{1,0:T(8,128)} fusion(bf16[2,1024,2048]{2,1,0:T(8,128)(2,1)} %copy-done.6, bf16[2,1024,2048]{2,1,0:T(8,128)(2,1)} %dynamic-slice_multiply_fusion), kind=kOutput, calls=%fused_computation.48 | convolution fusion | flops 17179869184 | bytes 33554432 | tf_op jit(solution)/shard_map/dot_general | solution.py:40
  580.6 11.9 multiply_reduce_fusion
  592.5 15.6 multiply_convert_fusion
  642.4 33.5 %convert_reduce_fusion.1 = (f32[2048]{0:T(1024)}, bf16[2,1024,2048]{2,1,0:T(8,128)(2,1)S(1)}) fusion(f32[2,1024,2048]{2,1,0:T(8,128)} %get-tuple-element.44, bf16[2,1024,2048]{2,1,0:T(8,128)(2,1)} %dynamic-slice_multiply_fusion, bf16[2048,2048]{1,0:T(8,128)(2,1)} %param.28, f32[2,1024,2048]{2,1,0:T(8,128)} %get-tuple-element.81, f32[2048]{0:T(1024)S(1)} %copy-done.17), kind=kOutput, calls=%fused_computation.23 | convolution fusion | flops 17251170304 | bytes 58736640 | tf_op jit(solution)/shard_map/dot_general | solution.py:40
  679.2 22.7 %convolution_bitcast_fusion.1 = f32[2048,2048]{1,0:T(8,128)} fusion(bf16[2,1024,2048]{2,1,0:T(8,128)(2,1)S(1)} %get-tuple-element.27, bf16[2,1024,2048]{2,1,0:T(8,128)(2,1)} %constant_dynamic-slice_fusion.2, f32[2048]{0:T(1024)S(1)} %copy-done.31, f32[2048]{0:T(1024)S(1)} %copy-done.25, f32[2,1024]{1,0:T(2,128)S(1)} %copy-done.33, f32[2,1024]{1,0:T(2,128)S(1)} %copy-done.19), kind=kOutput, calls=%fused_computation.47 | convolution fusion | flops 17205035008 | bytes 33587200 | tf_op jit(solution)/shard_map/dot_general | solution.py:40
  701.9 22.2 %convolution_bitcast_fusion = f32[2048,1536]{1,0:T(8,128)} fusion(bf16[2,1024,1536]{1,2,0:T(8,128)(2,1)} %bitcast.105, bf16[2,1024,2048]{2,1,0:T(8,128)(2,1)} %constant_dynamic-slice_fusion.2, f32[2048]{0:T(1024)S(1)} %copy-done.29, f32[2048]{0:T(1024)S(1)} %copy-done.27, f32[2,1024]{1,0:T(2,128)S(1)} %copy-done.33, f32[2,1024]{1,0:T(2,128)S(1)} %copy-done.19), kind=kOutput, calls=%fused_computation.46 | convolution fusion | flops 12910067712 | bytes 27295744 | tf_op jit(solution)/shard_map/dot_general | solution.py:40
  724.1 21.0 %fusion.34 = f32[2,1024,2048]{2,1,0:T(8,128)} fusion(bf16[2,1024,1536]{1,2,0:T(8,128)(2,1)} %bitcast.106, bf16[2048,1536]{1,0:T(8,128)(2,1)} %param.22), kind=kOutput, calls=%fused_computation.63 | convolution fusion | flops 12884901888 | bytes 29360128 | tf_op jit(solution)/shard_map/dot_general | solution.py:40
  758.0 31.8 %fusion.80 = (f32[2048]{0:T(1024)S(1)}, f32[2048]{0:T(1024)S(1)}, f32[2,1024,2048]{2,1,0:T(8,128)}, f32[2048]{0:T(1024)S(1)}, f32[2048]{0:T(1024)S(1)}) fusion(f32[2,1024]{1,0:T(2,128)S(1)} %copy-done.33, f32[2,1024]{1,0:T(2,128)S(1)} %copy-done.19, bf16[2,1024,2048]{2,1,0:T(8,128)(2,1)} %constant_dynamic-slice_fusion.2, f32[2048]{0:T(1024)S(1)} %copy-done.25, ...), kind=kOutput, calls=%fused_computation.157 | convolution fusion | flops 17230192640 | bytes 58785792 | tf_op jit(solution)/shard_map/dot_general | solution.py:40
  808.7 29.4 %collective-permute-done.18 = bf16[2,256,2048]{2,1,0:T(8,128)(2,1)} collective-permute-done((bf16[2,256,2048]{2,1,0:T(8,128)(2,1)}, bf16[2,256,2048]{2,1,0:T(8,128)(2,1)}, u32[]{:S(2)}, u32[]{:S(2)}) %collective-permute-start.18) | collective-permute-done | bytes 2097184 | tf_op jit(solution)/shard_map/ppermute | solution.py:75
  848.6 37.6 %collective-permute-done.19 = bf16[2,256,2048]{2,1,0:T(8,128)(2,1)} collective-permute-done((bf16[2,256,2048]{2,1,0:T(8,128)(2,1)S(1)}, bf16[2,256,2048]{2,1,0:T(8,128)(2,1)}, u32[]{:S(2)}, u32[]{:S(2)}) %collective-permute-start.19) | collective-permute-done | bytes 2097184 | tf_op jit(solution)/shard_map/ppermute | solution.py:75
  894.4 11.1 collective-permute-start.8
  913.5 45.3 %collective-permute-start.20 = (bf16[2,256,2048]{2,1,0:T(8,128)(2,1)}, bf16[2,256,2048]{2,1,0:T(8,128)(2,1)}, u32[]{:S(2)}, u32[]{:S(2)}) collective-permute-start(bf16[2,256,2048]{2,1,0:T(8,128)(2,1)} %get-tuple-element.48), channel_id=1, source_target_pairs={{0,1},{1,2},{2,3},{4,5},{5,6},{6,7},{8,9},{9,10},{10,11},{12,13},{... | collective-permute-start | bytes 6291464 | tf_op jit(solution)/shard_map/ppermute | solution.py:75
  968.8 59.1 %collective-permute-done.20 = bf16[2,256,2048]{2,1,0:T(8,128)(2,1)} collective-permute-done((bf16[2,256,2048]{2,1,0:T(8,128)(2,1)}, bf16[2,256,2048]{2,1,0:T(8,128)(2,1)}, u32[]{:S(2)}, u32[]{:S(2)}) %collective-permute-start.20) | collective-permute-done | bytes 2097184 | tf_op jit(solution)/shard_map/ppermute | solution.py:75
  1027.9 39.2 %collective-permute-done.23 = bf16[2,256,2048]{2,1,0:T(8,128)(2,1)} collective-permute-done((bf16[2,256,2048]{2,1,0:T(8,128)(2,1)}, bf16[2,256,2048]{2,1,0:T(8,128)(2,1)}, u32[]{:S(2)}, u32[]{:S(2)}) %collective-permute-start.23) | collective-permute-done | bytes 2097184 | tf_op jit(solution)/shard_map/ppermute | solution.py:78
  1085.6 23.1 %reduce-scatter.26.cloned.1.call-done = f32[256,1]{1,0:T(8,128)} async-done(((f32[2048,1]{1,0:T(8,128)}), f32[256,1]{1,0:T(8,128)}) %reduce-scatter.26.cloned.1.call-update) | async-done | bytes 1040
  1110.3 194.5 %reduce-scatter.22.cloned.1.call-done = f32[64,5]{1,0:T(8,128)} async-done(((f32[2048,5]{1,0:T(8,128)}), f32[64,5]{1,0:T(8,128)}) %reduce-scatter.22.cloned.1.call-update) | async-done | bytes 1296
  1308.3 47.7 %reduce-scatter.16.cloned.1.call-done = f32[512,256]{1,0:T(8,128)} async-done(((f32[512,2048]{1,0:T(8,128)}), f32[512,256]{1,0:T(8,128)}) %reduce-scatter.16.cloned.1.call-update) | async-done | bytes 524304 | tf_op jit(solution)/shard_map/reduce_scatter | solution.py:221
  1356.1 96.2 %reduce-scatter.14.cloned.1.call-done = f32[256,1536]{1,0:T(8,128)} async-done(((f32[2048,1536]{1,0:T(8,128)}), f32[256,1536]{1,0:T(8,128)}) %reduce-scatter.14.cloned.1.call-update) | async-done | bytes 1572880 | tf_op jit(solution)/shard_map/reduce_scatter | solution.py:220
  1452.3 120.2 %reduce-scatter.18.cloned.1.call-done = f32[256,2048]{1,0:T(8,128)} async-done(((f32[2048,2048]{1,0:T(8,128)}), f32[256,2048]{1,0:T(8,128)}) %reduce-scatter.18.cloned.1.call-update) | async-done | bytes 2097168 | tf_op jit(solution)/shard_map/reduce_scatter | solution.py:222
  1572.5 120.2 %reduce-scatter.20.cloned.1.call-done = f32[2048,256]{1,0:T(8,128)} async-done(((f32[2048,2048]{1,0:T(8,128)}), f32[2048,256]{1,0:T(8,128)}) %reduce-scatter.20.cloned.1.call-update) | async-done | bytes 2097168 | tf_op jit(solution)/shard_map/reduce_scatter | solution.py:223
  (219 shorter events, 327.0 us)
Async XLA Ops:
  7.2 1077.0 %reduce-scatter.24.cloned.1.call-start = ((), (), s32[]{:S(2)}) async-start(), calls=%async_computation.12 | async-start | bytes 442368
  7.2 50.3 %collective-permute-start = (bf16[2,256,2048]{2,1,0:T(8,128)(2,1)}, bf16[2,256,2048]{2,1,0:T(8,128)(2,1)S(1)}, u32[]{:S(2)}, u32[]{:S(2)}) collective-permute-start(bf16[2,256,2048]{2,1,0:T(8,128)(2,1)} %param.15), channel_id=1, source_target_pairs={{0,1},{1,2},{2,3},{4,5},{5,6},{6,7},{8,9},{9,10},{10,11},{12,13},{... | collective-permute-start | bytes 6291464 | tf_op jit(solution)/shard_map/ppermute | solution.py:50
  12.5 49.3 %collective-permute-start.3 = (bf16[2,256,2048]{2,1,0:T(8,128)(2,1)}, bf16[2,256,2048]{2,1,0:T(8,128)(2,1)}, u32[]{:S(2)}, u32[]{:S(2)}) collective-permute-start(bf16[2,256,2048]{2,1,0:T(8,128)(2,1)} %param.15), channel_id=1, source_target_pairs={{1,0},{2,1},{3,2},{5,4},{6,5},{7,6},{9,8},{10,9},{11,10},{13,12},{... | collective-permute-start | bytes 6291464 | tf_op jit(solution)/shard_map/ppermute | solution.py:51
  58.8 4.2 collective-permute-start.1
  61.8 51.1 %collective-permute-start.4 = (bf16[2,256,2048]{2,1,0:T(8,128)(2,1)}, bf16[2,256,2048]{2,1,0:T(8,128)(2,1)}, u32[]{:S(2)}, u32[]{:S(2)}) collective-permute-start(bf16[2,256,2048]{2,1,0:T(8,128)(2,1)} %collective-permute-done.3), channel_id=1, source_target_pairs={{1,0},{2,1},{5,4},{6,5},{9,8},{10,9},{13,12},{14,13},{17,16},{18,1... | collective-permute-start | bytes 6291464 | tf_op jit(solution)/shard_map/ppermute | solution.py:51
  63.1 55.0 %collective-permute-start.2 = (bf16[2,256,2048]{2,1,0:T(8,128)(2,1)}, bf16[2,256,2048]{2,1,0:T(8,128)(2,1)}, u32[]{:S(2)}, u32[]{:S(2)}) collective-permute-start(bf16[2,256,2048]{2,1,0:T(8,128)(2,1)} %collective-permute-done.1), channel_id=1, source_target_pairs={{2,3},{6,7},{10,11},{14,15},{18,19},{22,23},{26,27},{30,31}} | collective-permute-start | bytes 6291464 | tf_op jit(solution)/shard_map/ppermute | solution.py:50
  112.8 48.0 %collective-permute-start.5 = (bf16[2,256,2048]{2,1,0:T(8,128)(2,1)}, bf16[2,256,2048]{2,1,0:T(8,128)(2,1)S(1)}, u32[]{:S(2)}, u32[]{:S(2)}) collective-permute-start(bf16[2,256,2048]{2,1,0:T(8,128)(2,1)} %collective-permute-done.4), channel_id=1, source_target_pairs={{1,0},{5,4},{9,8},{13,12},{17,16},{21,20},{25,24},{29,28}} | collective-permute-start | bytes 6291464 | tf_op jit(solution)/shard_map/ppermute | solution.py:51
  170.7 229.6 %collective-permute-start.12 = (bf16[2,256,2048]{2,1,0:T(8,128)(2,1)}, bf16[2,256,2048]{2,1,0:T(8,128)(2,1)}, u32[]{:S(2)}, u32[]{:S(2)}) collective-permute-start(bf16[2,256,2048]{2,1,0:T(8,128)(2,1)} %param.17), channel_id=1, source_target_pairs={{0,1},{1,2},{2,3},{4,5},{5,6},{6,7},{8,9},{9,10},{10,11},{12,13},{... | collective-permute-start | bytes 6291464 | tf_op jit(solution)/shard_map/ppermute | solution.py:50
  174.0 228.3 %collective-permute-start.15 = (bf16[2,256,2048]{2,1,0:T(8,128)(2,1)}, bf16[2,256,2048]{2,1,0:T(8,128)(2,1)}, u32[]{:S(2)}, u32[]{:S(2)}) collective-permute-start(bf16[2,256,2048]{2,1,0:T(8,128)(2,1)} %param.17), channel_id=1, source_target_pairs={{1,0},{2,1},{3,2},{5,4},{6,5},{7,6},{9,8},{10,9},{11,10},{13,12},{... | collective-permute-start | bytes 6291464 | tf_op jit(solution)/shard_map/ppermute | solution.py:51
  383.9 101.7 %collective-permute-start.6 = (f32[2,256,2048]{2,1,0:T(8,128)}, f32[2,256,2048]{2,1,0:T(8,128)}, u32[]{:S(2)}, u32[]{:S(2)}) collective-permute-start(f32[2,256,2048]{2,1,0:T(8,128)} %constant_dynamic-slice_fusion.1), channel_id=1, source_target_pairs={{0,1},{4,5},{8,9},{12,13},{16,17},{20,21},{24,25},{28,29}} | collective-permute-start | bytes 12582920 | tf_op jit(solution)/shard_map/ppermute | solution.py:75
  400.3 3.2 collective-permute-start.13
  402.3 47.2 %collective-permute-start.16 = (bf16[2,256,2048]{2,1,0:T(8,128)(2,1)}, bf16[2,256,2048]{2,1,0:T(8,128)(2,1)}, u32[]{:S(2)}, u32[]{:S(2)}) collective-permute-start(bf16[2,256,2048]{2,1,0:T(8,128)(2,1)} %collective-permute-done.15), channel_id=1, source_target_pairs={{1,0},{2,1},{5,4},{6,5},{9,8},{10,9},{13,12},{14,13},{17,16},{18,1... | collective-permute-start | bytes 6291464 | tf_op jit(solution)/shard_map/ppermute | solution.py:51
  403.6 94.9 %collective-permute-start.14 = (bf16[2,256,2048]{2,1,0:T(8,128)(2,1)}, bf16[2,256,2048]{2,1,0:T(8,128)(2,1)}, u32[]{:S(2)}, u32[]{:S(2)}) collective-permute-start(bf16[2,256,2048]{2,1,0:T(8,128)(2,1)} %collective-permute-done.13), channel_id=1, source_target_pairs={{2,3},{6,7},{10,11},{14,15},{18,19},{22,23},{26,27},{30,31}} | collective-permute-start | bytes 6291464 | tf_op jit(solution)/shard_map/ppermute | solution.py:50
  449.5 68.3 %collective-permute-start.17 = (bf16[2,256,2048]{2,1,0:T(8,128)(2,1)}, bf16[2,256,2048]{2,1,0:T(8,128)(2,1)S(1)}, u32[]{:S(2)}, u32[]{:S(2)}) collective-permute-start(bf16[2,256,2048]{2,1,0:T(8,128)(2,1)} %collective-permute-done.16), channel_id=1, source_target_pairs={{1,0},{5,4},{9,8},{13,12},{17,16},{21,20},{25,24},{29,28}} | collective-permute-start | bytes 6291464 | tf_op jit(solution)/shard_map/ppermute | solution.py:51
  492.2 253.0 %collective-permute-start.7 = (f32[2,256,2048]{2,1,0:T(8,128)}, f32[2,256,2048]{2,1,0:T(8,128)}, u32[]{:S(2)}, u32[]{:S(2)}) collective-permute-start(f32[2,256,2048]{2,1,0:T(8,128)} %dynamic-slice_add_fusion.2), channel_id=1, source_target_pairs={{0,1},{1,2},{4,5},{5,6},{8,9},{9,10},{12,13},{13,14},{16,17},{17,1... | collective-permute-start | bytes 12582920 | tf_op jit(solution)/shard_map/ppermute | solution.py:75
  755.3 43.6 %collective-permute-start.9 = (f32[2,256,2048]{2,1,0:T(8,128)}, f32[2,256,2048]{2,1,0:T(8,128)}, u32[]{:S(2)}, u32[]{:S(2)}) collective-permute-start(f32[2,256,2048]{2,1,0:T(8,128)} %get-tuple-element.53), channel_id=1, source_target_pairs={{3,2},{7,6},{11,10},{15,14},{19,18},{23,22},{27,26},{31,30}} | collective-permute-start | bytes 12582920 | tf_op jit(solution)/shard_map/ppermute | solution.py:78
  795.3 42.8 %collective-permute-start.18 = (bf16[2,256,2048]{2,1,0:T(8,128)(2,1)}, bf16[2,256,2048]{2,1,0:T(8,128)(2,1)}, u32[]{:S(2)}, u32[]{:S(2)}) collective-permute-start(bf16[2,256,2048]{2,1,0:T(8,128)(2,1)} %get-tuple-element.50), channel_id=1, source_target_pairs={{0,1},{4,5},{8,9},{12,13},{16,17},{20,21},{24,25},{28,29}} | collective-permute-start | bytes 6291464 | tf_op jit(solution)/shard_map/ppermute | solution.py:75
  797.9 49.4 %collective-permute-start.21 = (bf16[2,256,2048]{2,1,0:T(8,128)(2,1)S(1)}, bf16[2,256,2048]{2,1,0:T(8,128)(2,1)S(1)}, u32[]{:S(2)}, u32[]{:S(2)}) collective-permute-start(bf16[2,256,2048]{2,1,0:T(8,128)(2,1)S(1)} %get-tuple-element.51), channel_id=1, source_target_pairs={{3,2},{7,6},{11,10},{15,14},{19,18},{23,22},{27,26},{31,30}} | collective-permute-start | bytes 6291464 | tf_op jit(solution)/shard_map/ppermute | solution.py:78
  805.9 99.6 %collective-permute-start.10 = (f32[2,256,2048]{2,1,0:T(8,128)}, f32[2,256,2048]{2,1,0:T(8,128)}, u32[]{:S(2)}, u32[]{:S(2)}) collective-permute-start(f32[2,256,2048]{2,1,0:T(8,128)} %dynamic-slice_add_fusion), channel_id=1, source_target_pairs={{2,1},{3,2},{6,5},{7,6},{10,9},{11,10},{14,13},{15,14},{18,17},{19... | collective-permute-start | bytes 12582920 | tf_op jit(solution)/shard_map/ppermute | solution.py:78
  841.6 44.7 %collective-permute-start.19 = (bf16[2,256,2048]{2,1,0:T(8,128)(2,1)S(1)}, bf16[2,256,2048]{2,1,0:T(8,128)(2,1)}, u32[]{:S(2)}, u32[]{:S(2)}) collective-permute-start(bf16[2,256,2048]{2,1,0:T(8,128)(2,1)S(1)} %add_convert_fusion.4), channel_id=1, source_target_pairs={{0,1},{1,2},{4,5},{5,6},{8,9},{9,10},{12,13},{13,14},{16,17},{17,1... | collective-permute-start | bytes 6291464 | tf_op jit(solution)/shard_map/ppermute | solution.py:75
  892.3 66.5 %collective-permute-start.22 = (bf16[2,256,2048]{2,1,0:T(8,128)(2,1)}, bf16[2,256,2048]{2,1,0:T(8,128)(2,1)}, u32[]{:S(2)}, u32[]{:S(2)}) collective-permute-start(bf16[2,256,2048]{2,1,0:T(8,128)(2,1)} %get-tuple-element.49), channel_id=1, source_target_pairs={{2,1},{3,2},{6,5},{7,6},{10,9},{11,10},{14,13},{15,14},{18,17},{19... | collective-permute-start | bytes 6291464 | tf_op jit(solution)/shard_map/ppermute | solution.py:78
  894.4 177.1 %collective-permute-start.8 = (f32[2,256,2048]{2,1,0:T(8,128)}, f32[2,256,2048]{2,1,0:T(8,128)}, u32[]{:S(2)}, u32[]{:S(2)}) collective-permute-start(f32[2,256,2048]{2,1,0:T(8,128)} %get-tuple-element.52), channel_id=1, source_target_pairs={{0,1},{1,2},{2,3},{4,5},{5,6},{6,7},{8,9},{9,10},{10,11},{12,13},{... | collective-permute-start | bytes 12582920 | tf_op jit(solution)/shard_map/ppermute | solution.py:75
  912.1 159.4 %collective-permute-start.11 = (f32[2,256,2048]{2,1,0:T(8,128)}, f32[2,256,2048]{2,1,0:T(8,128)}, u32[]{:S(2)}, u32[]{:S(2)}) collective-permute-start(f32[2,256,2048]{2,1,0:T(8,128)} %dynamic-slice_add_fusion.1), channel_id=1, source_target_pairs={{1,0},{2,1},{3,2},{5,4},{6,5},{7,6},{9,8},{10,9},{11,10},{13,12},{... | collective-permute-start | bytes 12582920 | tf_op jit(solution)/shard_map/ppermute | solution.py:78
  913.5 114.4 %collective-permute-start.20 = (bf16[2,256,2048]{2,1,0:T(8,128)(2,1)}, bf16[2,256,2048]{2,1,0:T(8,128)(2,1)}, u32[]{:S(2)}, u32[]{:S(2)}) collective-permute-start(bf16[2,256,2048]{2,1,0:T(8,128)(2,1)} %get-tuple-element.48), channel_id=1, source_target_pairs={{0,1},{1,2},{2,3},{4,5},{5,6},{6,7},{8,9},{9,10},{10,11},{12,13},{... | collective-permute-start | bytes 6291464 | tf_op jit(solution)/shard_map/ppermute | solution.py:75
  963.7 103.5 %collective-permute-start.23 = (bf16[2,256,2048]{2,1,0:T(8,128)(2,1)}, bf16[2,256,2048]{2,1,0:T(8,128)(2,1)}, u32[]{:S(2)}, u32[]{:S(2)}) collective-permute-start(bf16[2,256,2048]{2,1,0:T(8,128)(2,1)} %add_convert_fusion.1), channel_id=1, source_target_pairs={{1,0},{2,1},{3,2},{5,4},{6,5},{7,6},{9,8},{10,9},{11,10},{13,12},{... | collective-permute-start | bytes 6291464 | tf_op jit(solution)/shard_map/ppermute | solution.py:78
  967.2 141.6 %reduce-scatter.26.cloned.1.call-start = ((), (), s32[]{:S(2)}) async-start(), calls=%async_computation.13 | async-start | bytes 1179648
  968.7 336.0 %reduce-scatter.22.cloned.1.call-start = ((), (), s32[]{:S(2)}) async-start(), calls=%async_computation.11 | async-start | bytes 1081344
  1081.7 274.4 %reduce-scatter.16.cloned.1.call-start = ((), (), s32[]{:S(2)}) async-start(), calls=%async_computation.8 | async-start | bytes 4718592 | tf_op jit(solution)/shard_map/reduce_scatter | solution.py:221
  1082.2 370.0 %reduce-scatter.14.cloned.1.call-start = ((), (), s32[]{:S(2)}) async-start(), calls=%async_computation.7 | async-start | bytes 14155776 | tf_op jit(solution)/shard_map/reduce_scatter | solution.py:220
  1082.8 489.7 %reduce-scatter.18.cloned.1.call-start = ((), (), s32[]{:S(2)}) async-start(), calls=%async_computation.9 | async-start | bytes 18874368 | tf_op jit(solution)/shard_map/reduce_scatter | solution.py:222
  1083.4 609.8 %copy-start.1 = (bf16[512,2048]{1,0:T(8,128)(2,1)S(1)}, bf16[512,2048]{1,0:T(8,128)(2,1)}, u32[]{:S(2)}) copy-start(bf16[512,2048]{1,0:T(8,128)(2,1)} %param.24) | copy-start | bytes 6291460
  1083.4 609.2 %reduce-scatter.20.cloned.1.call-start = ((), (), s32[]{:S(2)}) async-start(), calls=%async_computation.10 | async-start | bytes 18874368 | tf_op jit(solution)/shard_map/reduce_scatter | solution.py:223
  (42 other events, 2821.6 us)
Sparse Core Ops, SparseCore 0:
  967.3 102.2 reduce-scatter.23
  1072.8 35.9 reduce-scatter.25
  1111.0 193.7 reduce-scatter.21
  1308.6 47.4 reduce-scatter.15
  1360.0 92.2 reduce-scatter.13
  1456.3 116.1 reduce-scatter.17
  1576.6 115.9 reduce-scatter.19
